TPU v7x, 256 devices: a whole 4x4x8 slice. The times are simulated.
256 devices in a mesh: tm: 2 (over core), scen: 4 (over x), line: 32 (over z, y).
Axes of the slice: x: 4, y: 4, z: 8, core: 2. Of those that a mesh axis runs over, the one named last changes fastest.
Arguments:
- line_blocks: bfloat16 [64, 128, 1024], P('line'), may hold values from -0.1875 to 0.1875
- binding: int32 [128, 2, 8], P(('scen', 'line'), 'tm'), may hold values from 0 to 63, as said below
- line_weight: float32 [128, 2, 8, 128], P(('scen', 'line'), 'tm'), may hold values from 0.25 to 4
- barrier: float32 [128, 2, 1024], P(('scen', 'line'), 'tm'), may hold values from 0.5 to 4
- gradient: float32 [128, 2, 1024], P(('scen', 'line'), 'tm'), may hold values from -6 to 6
- link_columns: bfloat16 [128, 2, 1024, 128], P(('scen', 'line'), 'tm'), may hold values from -0.5 to 0.5
- ramp_weight: float32 [256], replicated, may hold values from 10 to 200
- link_diag: float32 [128], replicated, may hold values from 0.5 to 5
- link_rhs: float32 [128], replicated, may hold values from -18 to 18
Outputs:
- newton_step: float32 [128, 2, 1024], P(('scen', 'line'), 'tm')
- link_step: float32 [128], replicated
Inputs may be any that keep to these rules, and one draw needn't show every extreme that they name: Block numbers b are held by line device b // 2. Take the list binding[s, t] of one scenario s and period t: exactly one line device holds 2 of its blocks, no line device holds more, and the other blocks are spread as evenly as possible over the other line devices, in a shuffled order. A block may appear more than once.
All inputs are finite; a program needn't handle non-finite values.
Results may differ from a plain program's by a relative error of at most 0.00084.
Values may be sent and summed in bfloat16 or wider, within the bound.
No kernel may reach another device: no remote copies, remote signals or barrier semaphores. Data moves between devices by JAX's collectives and lax.ppermute only.
A program may use at most 128 MiB of HBM per device.

v0:
```python
import jax
import jax.numpy as jnp
from jax import lax
from jax.sharding import PartitionSpec as P

highest = lax.Precision.HIGHEST


def period_hessian(selected, weights, barrier_row, ramp_weight, end_factor):
    order = selected.shape[-1]
    scaled = (weights[:, :, None] * selected.astype(jnp.float32)).astype(jnp.bfloat16)
    flat = selected.reshape(-1, order)
    scaled_flat = scaled.reshape(-1, order)
    hessian = lax.dot_general(
        flat, scaled_flat, (((0,), (0,)), ((), ())), preferred_element_type=jnp.float32
    )
    count = ramp_weight.shape[0]
    extra = jnp.concatenate([end_factor * ramp_weight, jnp.zeros((order - count,), jnp.float32)])
    return hessian + jnp.diag(barrier_row + extra)


def butterfly_sum(value, axes):
    for axis in axes:
        size = lax.axis_size(axis)
        step = 1
        while step < size:
            pairs = [(i, i ^ step) for i in range(size)]
            value = value + lax.ppermute(value, axis, pairs)
            step *= 2
    return value


def trsm(a, b, transpose=False):
    return lax.linalg.triangular_solve(a, b, left_side=True, lower=True, transpose_a=transpose)


def on_device(
    line_blocks,
    binding,
    line_weight,
    barrier,
    gradient,
    link_columns,
    ramp_weight,
    link_diag,
    link_rhs,
):
    block_ids = binding[0, 0]
    order = line_blocks.shape[2]
    count = ramp_weight.shape[0]
    links = link_columns.shape[-1]
    every_block = lax.all_gather(line_blocks, "line", axis=0, tiled=True)
    selected = jnp.take(every_block, block_ids, axis=0)
    shard = lax.axis_index("tm")
    shards = lax.axis_size("tm")
    end_factor = jnp.where((shard == 0) | (shard == shards - 1), 1.0, 2.0).astype(jnp.float32)
    hessian = period_hessian(selected, line_weight[0, 0], barrier[0, 0], ramp_weight, end_factor)

    link_float = link_columns[0, 0].astype(jnp.float32)
    rhs = jnp.concatenate([gradient[0, 0][:, None], link_float], axis=1)

    h_nn = hessian[count:, count:]
    h_nr = hessian[count:, :count]
    h_rr = hessian[:count, :count]
    l_nn = lax.linalg.cholesky(h_nn)
    solved = trsm(l_nn, jnp.concatenate([h_nr, rhs[count:]], axis=1))
    x_nr = solved[:, :count]
    y_n = solved[:, count:]
    schur = h_rr - jnp.dot(x_nr.T, x_nr, precision=highest)
    reduced = rhs[:count] - jnp.dot(x_nr.T, y_n, precision=highest)

    mine = jnp.concatenate([schur, reduced], axis=1)
    other = lax.ppermute(mine, "tm", [(0, 1), (1, 0)])
    first = shard == 0
    part0 = jnp.where(first, mine, other)
    part1 = jnp.where(first, other, mine)
    coupling = -jnp.diag(ramp_weight)
    system = jnp.concatenate(
        [
            jnp.concatenate([part0[:, :count], coupling], axis=1),
            jnp.concatenate([coupling, part1[:, :count]], axis=1),
        ],
        axis=0,
    )
    lower = lax.linalg.cholesky(system)
    ramp_both = jax.scipy.linalg.cho_solve(
        (lower, True), jnp.concatenate([part0[:, count:], part1[:, count:]], axis=0)
    )
    x_r = jnp.where(first, ramp_both[:count], ramp_both[count:])
    x_n = trsm(l_nn, y_n - jnp.dot(x_nr, x_r, precision=highest), transpose=True)
    solution_cols = jnp.concatenate([x_r, x_n], axis=0)
    step_vec = solution_cols[:, 0]
    step_cols = solution_cols[:, 1:]

    local = jnp.dot(link_float.T, solution_cols, precision=highest)
    total = butterfly_sum(local, ("tm", "scen", "line"))
    vec_total = total[:, 0]
    mat_total = total[:, 1:]
    inverse_count = 1.0 / (shards * lax.axis_size("scen") * lax.axis_size("line"))
    link_system = jnp.diag(link_diag) + inverse_count * mat_total
    right_side = inverse_count * vec_total - link_rhs
    link_lower = jnp.linalg.cholesky(link_system)
    link_step = jax.scipy.linalg.cho_solve((link_lower, True), right_side)
    newton_step = step_vec - jnp.dot(step_cols, link_step, precision=highest)
    return (newton_step[None, None], link_step)


def solution(mesh):
    return jax.shard_map(
        on_device,
        mesh=mesh,
        in_specs=(
            P("line", None, None),
            P(("scen", "line"), "tm", None),
            P(("scen", "line"), "tm", None, None),
            P(("scen", "line"), "tm", None),
            P(("scen", "line"), "tm", None),
            P(("scen", "line"), "tm", None, None),
            P(),
            P(),
            P(),
        ),
        out_specs=(P(("scen", "line"), "tm", None), P()),
        check_vma=False,
    )
```

profile of v0, /device:TPU:2, one launch (start us, length us, event | category | flops | bytes accessed | tf_op | source)
XLA Modules:
  0.0 658.6 jit_solution(9514112737942022669)
XLA Ops:
  10.6 1.5 fusion.34
  12.1 141.1 %all-gather.2.cloned.1.call-done = bf16[64,128,1024]{2,1,0:T(8,128)(2,1)} async-done(((bf16[2,128,1024]{2,1,0:T(8,128)(2,1)}), bf16[64,128,1024]{2,1,0:T(8,128)(2,1)}) %all-gather.2.cloned.1.call-update) | async-done | bytes 16777232 | tf_op jit(solution)/shard_map/all_gather | solution.py:52
  153.3 6.4 gather_fusion
  159.7 2.6 bitcast_add_fusion
  162.4 1.8 slice.357
  165.0 2.3 copy.58
  167.3 2.0 fusion.1
  170.8 11.7 %cholesky.243 = f32[128,128]{1,0:T(8,128)S(1)} custom-call(f32[128,128]{1,0:T(8,128)S(1)} %copy.59), custom_call_target="Cholesky" | custom-call | tf_op jit(solution)/shard_map/cholesky | solution.py:65
  182.5 9.8 %custom-call.59 = f32[1,128,128]{1,2,0:T(8,128)S(1)} custom-call(f32[1,128,128]{2,1,0:T(8,128)S(1)} %get-tuple-element.78), custom_call_target="InvertDiagBlocksLowerTriangular" | custom-call | tf_op jit(solution)/shard_map/cholesky | solution.py:65
  192.5 1.7 constant_dynamic-update-slice_fusion.26
  194.2 1.4 convolution_subtract_fusion.1
  196.4 12.5 %cholesky.266 = f32[128,128]{1,0:T(8,128)S(1)} custom-call(f32[128,128]{1,0:T(8,128)} %copy.61), custom_call_target="Cholesky" | custom-call | tf_op jit(solution)/shard_map/cholesky | solution.py:65
  209.5 11.0 %custom-call.60 = f32[1,128,128]{1,2,0:T(8,128)S(1)} custom-call(f32[1,128,128]{2,1,0:T(8,128)} %get-tuple-element.75), custom_call_target="InvertDiagBlocksLowerTriangular" | custom-call | tf_op jit(solution)/shard_map/cholesky | solution.py:65
  221.2 1.6 convolution_subtract_fusion.3
  223.5 12.5 %cholesky.293 = f32[128,128]{1,0:T(8,128)S(1)} custom-call(f32[128,128]{1,0:T(8,128)} %copy.63), custom_call_target="Cholesky" | custom-call | tf_op jit(solution)/shard_map/cholesky | solution.py:65
  236.8 9.8 %custom-call.67 = f32[1,128,128]{1,2,0:T(8,128)S(1)} custom-call(f32[1,128,128]{2,1,0:T(8,128)S(1)} %get-tuple-element.72), custom_call_target="InvertDiagBlocksLowerTriangular" | custom-call | tf_op jit(solution)/shard_map/cholesky/custom-call.17 | solution.py:65
  247.1 1.6 convolution_subtract_fusion.10
  248.9 11.9 %cholesky.522 = f32[128,128]{1,0:T(8,128)S(1)} custom-call(f32[128,128]{1,0:T(8,128)S(1)} %copy.66), custom_call_target="Cholesky" | custom-call | tf_op jit(solution)/shard_map/cholesky | solution.py:65
  261.5 9.8 %custom-call.68 = f32[1,128,128]{1,2,0:T(8,128)S(1)} custom-call(f32[1,128,128]{2,1,0:T(8,128)S(1)} %get-tuple-element.69), custom_call_target="InvertDiagBlocksLowerTriangular" | custom-call | tf_op jit(solution)/shard_map/cholesky/custom-call.18 | solution.py:65
  271.7 1.6 convolution_subtract_fusion.13
  273.4 11.7 %cholesky.537 = f32[128,128]{1,0:T(8,128)S(1)} custom-call(f32[128,128]{1,0:T(8,128)S(1)} %copy.69), custom_call_target="Cholesky" | custom-call | tf_op jit(solution)/shard_map/cholesky | solution.py:65
  285.8 9.8 %custom-call.69 = f32[1,128,128]{1,2,0:T(8,128)S(1)} custom-call(f32[1,128,128]{2,1,0:T(8,128)S(1)} %get-tuple-element.66), custom_call_target="InvertDiagBlocksLowerTriangular" | custom-call | tf_op jit(solution)/shard_map/cholesky/custom-call.19 | solution.py:65
  297.3 12.1 %cholesky.551 = f32[128,128]{1,0:T(8,128)S(1)} custom-call(f32[128,128]{1,0:T(8,128)S(1)} %copy.72), custom_call_target="Cholesky" | custom-call | tf_op jit(solution)/shard_map/cholesky | solution.py:65
  314.6 1.6 select_select_fusion
  316.2 21.1 %while.2 = (s32[]{:T(128)}, f32[768,768]{1,0:T(8,128)}, s32[6,2]{0,1:T(2,128)S(1)}, f32[6,128,128]{2,1,0:T(8,128)}, s32[]{:T(128)}) while((s32[]{:T(128)}, f32[768,768]{1,0:T(8,128)}, s32[6,2]{0,1:T(2,128)S(1)}, f32[6,128,128]{2,1,0:T(8,128)}, s32[]{:T(128)}) %tuple.70), condition=%wide.while_cond, body=%wide.while_body.sunk | while | flops 2 | bytes 132705 | solution.py:34
  316.8 2.9 bitcast_dynamic-update-slice_fusion.4
  320.3 2.9 bitcast_dynamic-update-slice_fusion.4
  323.9 2.9 bitcast_dynamic-update-slice_fusion.4
  327.4 2.9 bitcast_dynamic-update-slice_fusion.4
  330.9 2.9 bitcast_dynamic-update-slice_fusion.4
  334.5 2.8 bitcast_dynamic-update-slice_fusion.4
  337.3 59.8 %custom-call.61 = f32[6,128,128]{1,2,0:T(8,128)S(1)} custom-call(f32[6,128,128]{2,1,0:T(8,128)} %get-tuple-element.12), custom_call_target="InvertDiagBlocksLowerTriangular" | custom-call | tf_op jit(solution)/shard_map/triangular_solve | solution.py:34
  397.1 1.4 constant_dynamic-update-slice_fusion.4
  402.2 1.7 convolution_subtract_fusion.4
  404.4 1.8 convolution_subtract_fusion.7
  406.7 2.1 convolution_subtract_fusion.8
  409.3 1.8 convolution_subtract_fusion.2
  412.4 1.7 collective-permute-done
  418.6 11.7 %cholesky.565 = f32[128,128]{1,0:T(8,128)S(1)} custom-call(f32[128,128]{1,0:T(8,128)S(1)} %cholesky.649), custom_call_target="Cholesky" | custom-call | tf_op jit(solution)/shard_map/cholesky | solution.py:85
  430.5 9.8 %custom-call.70 = f32[1,128,128]{1,2,0:T(8,128)S(1)} custom-call(f32[1,128,128]{2,1,0:T(8,128)S(1)} %get-tuple-element.62), custom_call_target="InvertDiagBlocksLowerTriangular" | custom-call | tf_op jit(solution)/shard_map/cholesky/custom-call.17 | solution.py:85
  442.9 11.7 %cholesky.576 = f32[128,128]{1,0:T(8,128)S(1)} custom-call(f32[128,128]{1,0:T(8,128)S(1)} %cholesky.653), custom_call_target="Cholesky" | custom-call | tf_op jit(solution)/shard_map/cholesky | solution.py:85
  455.9 10.2 %custom-call.71 = f32[1,128,128]{1,2,0:T(8,128)S(1)} custom-call(f32[1,128,128]{2,1,0:T(8,128)S(1)} %get-tuple-element.59), custom_call_target="InvertDiagBlocksLowerTriangular" | custom-call | tf_op jit(solution)/shard_map/cholesky/custom-call.18 | solution.py:85
  467.7 11.7 %cholesky.593 = f32[128,128]{1,0:T(8,128)S(1)} custom-call(f32[128,128]{1,0:T(8,128)S(1)} %cholesky.658), custom_call_target="Cholesky" | custom-call | tf_op jit(solution)/shard_map/cholesky | solution.py:85
  480.0 9.8 %custom-call.72 = f32[1,128,128]{1,2,0:T(8,128)S(1)} custom-call(f32[1,128,128]{2,1,0:T(8,128)S(1)} %get-tuple-element.56), custom_call_target="InvertDiagBlocksLowerTriangular" | custom-call | tf_op jit(solution)/shard_map/cholesky/custom-call.19 | solution.py:85
  491.3 11.9 %cholesky.606 = f32[128,128]{1,0:T(8,128)S(1)} custom-call(f32[128,128]{1,0:T(8,128)S(1)} %convolution_subtract_fusion.23), custom_call_target="Cholesky" | custom-call | tf_op jit(solution)/shard_map/cholesky | solution.py:85
  506.5 10.9 %while.3 = (s32[]{:T(128)}, f32[512,512]{1,0:T(8,128)S(1)}, s32[4,2]{0,1:T(2,128)S(1)}, f32[4,128,128]{2,1,0:T(8,128)}, s32[]{:T(128)}) while((s32[]{:T(128)}, f32[512,512]{1,0:T(8,128)S(1)}, s32[4,2]{0,1:T(2,128)S(1)}, f32[4,128,128]{2,1,0:T(8,128)}, s32[]{:T(128)}) %tuple.73), condition=%wide.while_cond.1, body=%wide.while_body.1.sunk | while | flops 2 | bytes 132705 | solution.py:86
  507.2 2.0 bitcast_dynamic-update-slice_fusion.5
  509.9 2.0 bitcast_dynamic-update-slice_fusion.5
  512.7 2.0 bitcast_dynamic-update-slice_fusion.5
  515.4 2.0 bitcast_dynamic-update-slice_fusion.5
  517.4 40.1 %custom-call.62 = f32[4,128,128]{1,2,0:T(8,128)S(1)} custom-call(f32[4,128,128]{2,1,0:T(8,128)} %get-tuple-element.20), custom_call_target="InvertDiagBlocksLowerTriangular" | custom-call | tf_op jit(solution)/shard_map/jit(_cho_solve)/triangular_solve | solution.py:86
  572.4 1.5 convolution_subtract_fusion.14
  576.9 5.0 collective-permute-done.2
  581.9 2.2 collective-permute-start.3
  584.1 4.4 collective-permute-done.3
  588.8 5.2 collective-permute-done.4
  595.3 5.4 collective-permute-done.5
  600.9 5.4 collective-permute-done.6
  606.2 1.9 collective-permute-start.7
  608.2 8.2 %collective-permute-done.7 = f32[128,129]{1,0:T(8,128)S(1)} collective-permute-done((f32[128,129]{1,0:T(8,128)S(1)}, f32[128,129]{1,0:T(8,128)S(1)}, u32[]{:S(2)}, u32[]{:S(2)}) %collective-permute-start.7) | collective-permute-done | bytes 66080 | tf_op jit(solution)/shard_map/ppermute | solution.py:28
  616.4 3.7 collective-permute-start.8
  620.2 6.6 %collective-permute-done.8 = f32[128,129]{1,0:T(8,128)S(1)} collective-permute-done((f32[128,129]{1,0:T(8,128)S(1)}, f32[128,129]{1,0:T(8,128)S(1)}, u32[]{:S(2)}, u32[]{:S(2)}) %collective-permute-start.8) | collective-permute-done | bytes 66080 | tf_op jit(solution)/shard_map/ppermute | solution.py:28
  627.2 11.7 %cholesky.617 = f32[128,128]{1,0:T(8,128)S(1)} custom-call(f32[128,128]{1,0:T(8,128)S(1)} %fusion.125), custom_call_target="Cholesky" | custom-call | tf_op jit(solution)/shard_map/jit(cholesky)/cholesky | solution.py:102
  640.3 9.8 %custom-call.63 = f32[1,128,128]{1,2,0:T(8,128)S(1)} custom-call(f32[1,128,128]{2,1,0:T(8,128)S(1)} %fusion.110), custom_call_target="InvertDiagBlocksLowerTriangular" | custom-call | tf_op jit(solution)/shard_map/jit(_cho_solve)/triangular_solve | solution.py:103
  (206 shorter events, 63.4 us)
Async XLA Ops:
  7.2 4.9 copy-start.21
  7.2 4.9 copy-start.15
  7.2 4.9 copy-start.16
  7.2 146.1 %all-gather.2.cloned.1.call-start = ((), (), s32[]{:S(2)}) async-start(), calls=%async_computation | async-start | bytes 17301504 | tf_op jit(solution)/shard_map/all_gather | solution.py:52
  9.8 0.8 copy-start.3
  10.6 149.1 %copy-start.20 = (f32[1,1,8,128]{3,2,1,0:T(8,128)S(1)}, f32[1,1,8,128]{3,2,1,0:T(8,128)}, u32[]{:S(2)}) copy-start(f32[1,1,8,128]{3,2,1,0:T(8,128)} %param.17) | copy-start | bytes 12292
  162.3 2.6 copy-start.1
  169.3 1.4 copy-start.2
  316.2 82.3 %copy-start = (f32[768,129]{0,1:T(8,128)S(1)}, f32[768,129]{0,1:T(8,128)}, u32[]{:S(2)}) copy-start(f32[768,129]{0,1:T(8,128)} %fusion.34) | copy-start | bytes 1188868
  397.0 11.7 %copy-start.11 = (f32[6,128,128]{1,2,0:T(8,128)}, f32[6,128,128]{1,2,0:T(8,128)S(1)}, u32[]{:S(2)}) copy-start(f32[6,128,128]{1,2,0:T(8,128)S(1)} %custom-call.61) | copy-start | bytes 1179652
  406.6 4.4 copy-start.4
  406.6 4.4 copy-start.14
  412.0 2.0 collective-permute-start
  412.4 2.7 copy-start.6
  414.1 0.8 copy-start.9
  414.1 0.9 copy-start.10
  414.2 1.0 copy-start.7
  415.1 0.7 copy-start.8
  417.6 1.0 copy-start.5
  561.6 4.3 copy-start.12
  567.3 6.9 %copy-start.13 = (bf16[1,1,1024,128]{3,2,1,0:T(8,128)(2,1)S(1)}, bf16[1,1,1024,128]{3,2,1,0:T(8,128)(2,1)}, u32[]{:S(2)}) copy-start(bf16[1,1,1024,128]{3,2,1,0:T(8,128)(2,1)} %param.20) | copy-start | bytes 786436
  574.2 52.7 %copy-start.17 = (f32[128]{0:T(128)S(1)}, f32[128]{0:T(128)}, u32[]{:S(2)}) copy-start(f32[128]{0:T(128)} %param.22) | copy-start | bytes 1540
  574.3 75.8 %copy-start.19 = (f32[128]{0:T(128)S(1)}, f32[128]{0:T(128)}, u32[]{:S(2)}) copy-start(f32[128]{0:T(128)} %param.23) | copy-start | bytes 1540
  574.8 1.4 collective-permute-start.1
  576.2 5.6 collective-permute-start.2
  581.9 6.6 collective-permute-start.3
  588.5 5.5 collective-permute-start.4
  594.0 6.8 %collective-permute-start.5 = (f32[128,129]{1,0:T(8,128)S(1)}, f32[128,129]{1,0:T(8,128)S(1)}, u32[]{:S(2)}, u32[]{:S(2)}) collective-permute-start(f32[128,129]{1,0:T(8,128)S(1)} %add.143), channel_id=1, source_target_pairs={{0,2},{1,3},{2,0},{3,1},{4,6},{5,7},{6,4},{7,5},{8,10},{9,11},{10,... | collective-permute-start | bytes 198152 | tf_op jit(solution)/shard_map/ppermute | solution.py:28
  600.8 5.5 collective-permute-start.6
  606.2 10.2 %collective-permute-start.7 = (f32[128,129]{1,0:T(8,128)S(1)}, f32[128,129]{1,0:T(8,128)S(1)}, u32[]{:S(2)}, u32[]{:S(2)}) collective-permute-start(f32[128,129]{1,0:T(8,128)S(1)} %add.145), channel_id=1, source_target_pairs={{0,8},{1,9},{2,10},{3,11},{4,12},{5,13},{6,14},{7,15},{8,0},{9,1},... | collective-permute-start | bytes 198152 | tf_op jit(solution)/shard_map/ppermute | solution.py:28
  616.4 10.4 %collective-permute-start.8 = (f32[128,129]{1,0:T(8,128)S(1)}, f32[128,129]{1,0:T(8,128)S(1)}, u32[]{:S(2)}, u32[]{:S(2)}) collective-permute-start(f32[128,129]{1,0:T(8,128)S(1)} %add.146), channel_id=1, source_target_pairs={{0,16},{1,17},{2,18},{3,19},{4,20},{5,21},{6,22},{7,23},{8,24},{9,... | collective-permute-start | bytes 198152 | tf_op jit(solution)/shard_map/ppermute | solution.py:28
  650.5 1.1 copy-start.18
Sparse Core Ops, SparseCore 0:
  10.6 142.6 all-gather.1
where the time goes:
time: 664 us; the launch traced here: 659 us
  other arithmetic  338 us (51%)
  waiting for transfers between devices  185 us (28%)
  local copies, waits for them, and re-layouts  52 us (8%)
  matrix products  51.5 us (8%)
  between operations  21.7 us (3%)
  starting transfers between devices  10.8 us (2%)
    all_gather x1, waiting for transfers between devices, on_device(): every_block = lax.all_gather(line_blocks, 'line', axis=0, tiled=True)  141 us
    another operation x22, other arithmetic, on_device(): l_nn = lax.linalg.cholesky(h_nn)  127 us
    another operation x15, other arithmetic, on_device(): lower = lax.linalg.cholesky(system)  79.5 us
    another operation x3, other arithmetic, trsm(): lax.linalg.triangular_solve(a, b, left_side=True, lower=True, transpose_a...  61.4 us
    ppermute x8, waiting for transfers between devices, butterfly_sum(): value = value + lax.ppermute(value, axis, pairs)  41.4 us
    another operation x3, other arithmetic, on_device(): jax.scipy.linalg.cho_solve((lower, True), jnp.concatenate([part0[:, count...  40.3 us
    another operation x30, local copies, waits for them, and re-layouts  32 us
    another operation x22, matrix products, trsm(): lax.linalg.triangular_solve(a, b, left_side=True, lower=True, transpose_a...  20.2 us
  transfers between devices with their start and end apart: 10, of which 10 were waited for; matrix products, arithmetic and copies ran while one was open for 1% of the time, Pallas kernels for 0%

commit v1 on v0

--- a/solution.py
+++ b/solution.py
@@ -49,10 +49,18 @@
     order = line_blocks.shape[2]
     count = ramp_weight.shape[0]
     links = link_columns.shape[-1]
-    every_block = lax.all_gather(line_blocks, "line", axis=0, tiled=True)
-    selected = jnp.take(every_block, block_ids, axis=0)
     shard = lax.axis_index("tm")
     shards = lax.axis_size("tm")
+    held = line_blocks.shape[0]
+    pairs = line_blocks.reshape((held // 2, 2) + line_blocks.shape[1:])
+    mine_half = lax.dynamic_index_in_dim(pairs, shard, axis=1, keepdims=False)
+    half = lax.all_gather(mine_half, "line", axis=0, tiled=True)
+    swap = [(0, 1), (1, 0)]
+    partner_ids = lax.ppermute(block_ids, "tm", swap)
+    for_partner = jnp.take(half, partner_ids // 2, axis=0)
+    from_partner = lax.ppermute(for_partner, "tm", swap)
+    own = jnp.take(half, block_ids // 2, axis=0)
+    selected = jnp.where((block_ids % 2 == shard)[:, None, None], own, from_partner)
     end_factor = jnp.where((shard == 0) | (shard == shards - 1), 1.0, 2.0).astype(jnp.float32)
     hessian = period_hessian(selected, line_weight[0, 0], barrier[0, 0], ramp_weight, end_factor)
 

time: 664 us -> 653 us (0.983)
  waiting for transfers between devices: 185 us -> 146 us
  matrix products: 51.5 us -> 65 us
  local copies, waits for them, and re-layouts: 52 us -> 60.2 us
    all_gather x1, waiting for transfers between devices: 141 us -> 101 us  [on_device(): half = lax.all_gather(mine_half, 'line', axis=0, tiled=True)]
  transfers between devices with their start and end apart: 10 -> 12, of which waited for: 10 -> 11; matrix products, arithmetic and copies ran while one was open for 1% -> 1% of each run, Pallas kernels for 0% -> 0%
where the time goes in v1:
time: 653 us; the launch traced here: 647 us
  other arithmetic  342 us (52%)
  waiting for transfers between devices  146 us (22%)
  matrix products  65 us (10%)
  local copies, waits for them, and re-layouts  60.2 us (9%)
  between operations  21.6 us (3%)
  starting transfers between devices  10.8 us (2%)
    another operation x22, other arithmetic, on_device(): l_nn = lax.linalg.cholesky(h_nn)  127 us
    all_gather x1, waiting for transfers between devices, on_device(): half = lax.all_gather(mine_half, 'line', axis=0, tiled=True)  101 us
    another operation x15, other arithmetic, on_device(): lower = lax.linalg.cholesky(system)  79.6 us
    another operation x3, other arithmetic, trsm(): lax.linalg.triangular_solve(a, b, left_side=True, lower=True, transpose_a...  63.7 us
    ppermute x8, waiting for transfers between devices, butterfly_sum(): value = value + lax.ppermute(value, axis, pairs)  42.7 us
    another operation x3, other arithmetic, on_device(): jax.scipy.linalg.cho_solve((lower, True), jnp.concatenate([part0[:, count...  41.2 us
    another operation x30, local copies, waits for them, and re-layouts  34.9 us
    another operation x22, matrix products, trsm(): lax.linalg.triangular_solve(a, b, left_side=True, lower=True, transpose_a...  20.1 us
  transfers between devices with their start and end apart: 12, of which 11 were waited for; matrix products, arithmetic and copies ran while one was open for 1% of the time, Pallas kernels for 0%

profile of v1, /device:TPU:2, one launch (start us, length us, event | category | flops | bytes accessed | tf_op | source)
XLA Modules:
  0.0 646.5 jit_solution(6177518466114886320)
XLA Ops:
  10.4 101.1 %all-gather.2.cloned.1.call-done = bf16[32,128,1024]{2,1,0:T(8,128)(2,1)} async-done(((bf16[1,128,1024]{2,1,0:T(8,128)(2,1)}), bf16[32,128,1024]{2,1,0:T(8,128)(2,1)}) %all-gather.2.cloned.1.call-update) | async-done | bytes 8388624 | tf_op jit(solution)/shard_map/all_gather | solution.py:57
  111.4 4.1 gather_fusion.1
  115.6 1.7 broadcast_select_fusion
  117.6 5.4 gather_fusion
  123.0 6.3 bitcast_add_fusion
  129.4 1.8 slice.359
  132.1 3.3 copy.58
  135.4 2.7 fusion.1
  139.6 11.7 %cholesky.243 = f32[128,128]{1,0:T(8,128)S(1)} custom-call(f32[128,128]{1,0:T(8,128)S(1)} %copy.59), custom_call_target="Cholesky" | custom-call | tf_op jit(solution)/shard_map/cholesky | solution.py:73
  151.4 9.8 %custom-call.59 = f32[1,128,128]{1,2,0:T(8,128)S(1)} custom-call(f32[1,128,128]{2,1,0:T(8,128)S(1)} %get-tuple-element.83), custom_call_target="InvertDiagBlocksLowerTriangular" | custom-call | tf_op jit(solution)/shard_map/cholesky | solution.py:73
  161.2 1.6 cholesky.277
  162.8 2.4 constant_dynamic-update-slice_fusion.26
  166.8 11.7 %cholesky.266 = f32[128,128]{1,0:T(8,128)S(1)} custom-call(f32[128,128]{1,0:T(8,128)S(1)} %copy.61), custom_call_target="Cholesky" | custom-call | tf_op jit(solution)/shard_map/cholesky | solution.py:73
  179.2 10.1 %custom-call.60 = f32[1,128,128]{1,2,0:T(8,128)S(1)} custom-call(f32[1,128,128]{2,1,0:T(8,128)S(1)} %get-tuple-element.80), custom_call_target="InvertDiagBlocksLowerTriangular" | custom-call | tf_op jit(solution)/shard_map/cholesky | solution.py:73
  190.6 1.9 slice_subtract_fusion.1
  192.6 11.7 %cholesky.293 = f32[128,128]{1,0:T(8,128)S(1)} custom-call(f32[128,128]{1,0:T(8,128)S(1)} %copy.63), custom_call_target="Cholesky" | custom-call | tf_op jit(solution)/shard_map/cholesky | solution.py:73
  205.6 9.8 %custom-call.67 = f32[1,128,128]{1,2,0:T(8,128)S(1)} custom-call(f32[1,128,128]{2,1,0:T(8,128)S(1)} %get-tuple-element.77), custom_call_target="InvertDiagBlocksLowerTriangular" | custom-call | tf_op jit(solution)/shard_map/cholesky/custom-call.17 | solution.py:73
  216.7 1.9 slice_subtract_fusion.3
  218.7 11.9 %cholesky.522 = f32[128,128]{1,0:T(8,128)S(1)} custom-call(f32[128,128]{1,0:T(8,128)S(1)} %copy.66), custom_call_target="Cholesky" | custom-call | tf_op jit(solution)/shard_map/cholesky | solution.py:73
  231.9 9.8 %custom-call.68 = f32[1,128,128]{1,2,0:T(8,128)S(1)} custom-call(f32[1,128,128]{2,1,0:T(8,128)S(1)} %get-tuple-element.74), custom_call_target="InvertDiagBlocksLowerTriangular" | custom-call | tf_op jit(solution)/shard_map/cholesky/custom-call.18 | solution.py:73
  242.8 1.8 slice_subtract_fusion.4
  244.8 11.7 %cholesky.537 = f32[128,128]{1,0:T(8,128)S(1)} custom-call(f32[128,128]{1,0:T(8,128)S(1)} %copy.69), custom_call_target="Cholesky" | custom-call | tf_op jit(solution)/shard_map/cholesky | solution.py:73
  257.8 9.8 %custom-call.69 = f32[1,128,128]{1,2,0:T(8,128)S(1)} custom-call(f32[1,128,128]{2,1,0:T(8,128)S(1)} %get-tuple-element.71), custom_call_target="InvertDiagBlocksLowerTriangular" | custom-call | tf_op jit(solution)/shard_map/cholesky/custom-call.19 | solution.py:73
  268.5 1.5 slice_subtract_fusion.11
  270.2 12.1 %cholesky.551 = f32[128,128]{1,0:T(8,128)S(1)} custom-call(f32[128,128]{1,0:T(8,128)S(1)} %copy.72), custom_call_target="Cholesky" | custom-call | tf_op jit(solution)/shard_map/cholesky | solution.py:73
  288.0 3.3 select_select_fusion
  291.3 21.1 %while.2 = (s32[]{:T(128)}, f32[768,768]{1,0:T(8,128)}, s32[6,2]{0,1:T(2,128)S(1)}, f32[6,128,128]{2,1,0:T(8,128)}, s32[]{:T(128)}) while((s32[]{:T(128)}, f32[768,768]{1,0:T(8,128)}, s32[6,2]{0,1:T(2,128)S(1)}, f32[6,128,128]{2,1,0:T(8,128)}, s32[]{:T(128)}) %tuple.74), condition=%wide.while_cond, body=%wide.while_body.sunk | while | flops 2 | bytes 132705 | solution.py:34
  292.0 2.9 bitcast_dynamic-update-slice_fusion.4
  295.5 2.9 bitcast_dynamic-update-slice_fusion.4
  299.0 2.9 bitcast_dynamic-update-slice_fusion.4
  302.5 2.9 bitcast_dynamic-update-slice_fusion.4
  306.1 2.9 bitcast_dynamic-update-slice_fusion.4
  309.6 2.8 bitcast_dynamic-update-slice_fusion.4
  312.4 60.4 %custom-call.61 = f32[6,128,128]{1,2,0:T(8,128)} custom-call(f32[6,128,128]{2,1,0:T(8,128)} %get-tuple-element.13), custom_call_target="InvertDiagBlocksLowerTriangular" | custom-call | tf_op jit(solution)/shard_map/triangular_solve | solution.py:34
  377.9 1.7 fusion.24
  380.1 1.8 fusion.12
  382.3 2.1 fusion.45
  384.9 1.8 slice_subtract_fusion.2
  388.4 1.5 collective-permute-done.2
  396.5 11.7 %cholesky.565 = f32[128,128]{1,0:T(8,128)S(1)} custom-call(f32[128,128]{1,0:T(8,128)S(1)} %cholesky.649), custom_call_target="Cholesky" | custom-call | tf_op jit(solution)/shard_map/cholesky | solution.py:93
  408.4 9.8 %custom-call.70 = f32[1,128,128]{1,2,0:T(8,128)S(1)} custom-call(f32[1,128,128]{2,1,0:T(8,128)S(1)} %get-tuple-element.67), custom_call_target="InvertDiagBlocksLowerTriangular" | custom-call | tf_op jit(solution)/shard_map/cholesky/custom-call.17 | solution.py:93
  420.7 11.7 %cholesky.576 = f32[128,128]{1,0:T(8,128)S(1)} custom-call(f32[128,128]{1,0:T(8,128)S(1)} %cholesky.653), custom_call_target="Cholesky" | custom-call | tf_op jit(solution)/shard_map/cholesky | solution.py:93
  433.8 10.2 %custom-call.71 = f32[1,128,128]{1,2,0:T(8,128)S(1)} custom-call(f32[1,128,128]{2,1,0:T(8,128)S(1)} %get-tuple-element.64), custom_call_target="InvertDiagBlocksLowerTriangular" | custom-call | tf_op jit(solution)/shard_map/cholesky/custom-call.18 | solution.py:93
  445.5 11.7 %cholesky.593 = f32[128,128]{1,0:T(8,128)S(1)} custom-call(f32[128,128]{1,0:T(8,128)S(1)} %cholesky.658), custom_call_target="Cholesky" | custom-call | tf_op jit(solution)/shard_map/cholesky | solution.py:93
  457.9 9.8 %custom-call.72 = f32[1,128,128]{1,2,0:T(8,128)S(1)} custom-call(f32[1,128,128]{2,1,0:T(8,128)S(1)} %get-tuple-element.61), custom_call_target="InvertDiagBlocksLowerTriangular" | custom-call | tf_op jit(solution)/shard_map/cholesky/custom-call.19 | solution.py:93
  469.1 11.9 %cholesky.606 = f32[128,128]{1,0:T(8,128)S(1)} custom-call(f32[128,128]{1,0:T(8,128)S(1)} %convolution_subtract_fusion.12), custom_call_target="Cholesky" | custom-call | tf_op jit(solution)/shard_map/cholesky | solution.py:93
  485.4 13.9 %while.3 = (s32[]{:T(128)}, f32[512,512]{1,0:T(8,128)}, s32[4,2]{0,1:T(2,128)S(1)}, f32[4,128,128]{2,1,0:T(8,128)}, s32[]{:T(128)}) while((s32[]{:T(128)}, f32[512,512]{1,0:T(8,128)}, s32[4,2]{0,1:T(2,128)S(1)}, f32[4,128,128]{2,1,0:T(8,128)}, s32[]{:T(128)}) %tuple.77), condition=%wide.while_cond.1, body=%wide.while_body.1.sunk | while | flops 2 | bytes 132705 | solution.py:94
  486.0 2.9 bitcast_dynamic-update-slice_fusion.5
  489.5 2.9 bitcast_dynamic-update-slice_fusion.5
  492.9 2.9 bitcast_dynamic-update-slice_fusion.5
  496.4 2.8 bitcast_dynamic-update-slice_fusion.5
  499.2 40.1 %custom-call.62 = f32[4,128,128]{1,2,0:T(8,128)S(1)} custom-call(f32[4,128,128]{2,1,0:T(8,128)} %get-tuple-element.21), custom_call_target="InvertDiagBlocksLowerTriangular" | custom-call | tf_op jit(solution)/shard_map/jit(_cho_solve)/triangular_solve | solution.py:94
  564.1 5.2 collective-permute-done.4
  569.3 2.2 collective-permute-start.5
  571.5 4.4 collective-permute-done.5
  576.2 5.0 collective-permute-done.6
  581.2 1.5 collective-permute-start.7
  582.7 5.2 collective-permute-done.7
  588.0 6.1 collective-permute-done.8
  595.4 8.9 %collective-permute-done.9 = f32[128,129]{1,0:T(8,128)S(1)} collective-permute-done((f32[128,129]{1,0:T(8,128)S(1)}, f32[128,129]{1,0:T(8,128)S(1)}, u32[]{:S(2)}, u32[]{:S(2)}) %collective-permute-start.9) | collective-permute-done | bytes 66080 | tf_op jit(solution)/shard_map/ppermute | solution.py:28
  604.3 3.4 collective-permute-start.10
  607.8 6.9 %collective-permute-done.10 = f32[128,129]{1,0:T(8,128)S(1)} collective-permute-done((f32[128,129]{1,0:T(8,128)S(1)}, f32[128,129]{1,0:T(8,128)S(1)}, u32[]{:S(2)}, u32[]{:S(2)}) %collective-permute-start.10) | collective-permute-done | bytes 66080 | tf_op jit(solution)/shard_map/ppermute | solution.py:28
  615.2 11.7 %cholesky.617 = f32[128,128]{1,0:T(8,128)S(1)} custom-call(f32[128,128]{1,0:T(8,128)S(1)} %fusion.155), custom_call_target="Cholesky" | custom-call | tf_op jit(solution)/shard_map/jit(cholesky)/cholesky | solution.py:110
  628.2 9.8 %custom-call.63 = f32[1,128,128]{1,2,0:T(8,128)S(1)} custom-call(f32[1,128,128]{2,1,0:T(8,128)S(1)} %fusion.136), custom_call_target="InvertDiagBlocksLowerTriangular" | custom-call | tf_op jit(solution)/shard_map/jit(_cho_solve)/triangular_solve | solution.py:111
  (208 shorter events, 78.8 us)
Async XLA Ops:
  7.2 1.0 copy-start
  7.2 104.3 %all-gather.2.cloned.1.call-start = ((), (), s32[]{:S(2)}) async-start(), calls=%async_computation | async-start | bytes 8650752 | tf_op jit(solution)/shard_map/all_gather | solution.py:57
  9.0 1.4 collective-permute-start
  115.5 1.7 copy-start.9
  115.5 1.9 copy-start.17
  115.5 2.0 copy-start.11
  115.5 2.0 copy-start.12
  115.6 2.0 copy-start.13
  117.2 5.8 collective-permute-start.1
  117.5 5.5 copy-start.18
  129.4 2.6 copy-start.1
  138.1 1.4 copy-start.2
  372.8 2.7 copy-start.7
  387.6 2.3 collective-permute-start.2
  391.0 0.8 copy-start.5
  391.0 0.9 copy-start.6
  391.9 0.7 copy-start.4
  395.5 1.0 copy-start.3
  545.2 8.0 %copy-start.8 = (f32[6,128,128]{1,2,0:T(8,128)S(1)}, f32[6,128,128]{1,2,0:T(8,128)}, u32[]{:S(2)}) copy-start(f32[6,128,128]{1,2,0:T(8,128)} %custom-call.61) | copy-start | bytes 1179652
  554.5 6.9 %copy-start.10 = (bf16[1,1,1024,128]{3,2,1,0:T(8,128)(2,1)S(1)}, bf16[1,1,1024,128]{3,2,1,0:T(8,128)(2,1)}, u32[]{:S(2)}) copy-start(bf16[1,1,1024,128]{3,2,1,0:T(8,128)(2,1)} %param.22) | copy-start | bytes 786436
  561.4 53.4 %copy-start.14 = (f32[128]{0:T(128)S(1)}, f32[128]{0:T(128)}, u32[]{:S(2)}) copy-start(f32[128]{0:T(128)} %param.24) | copy-start | bytes 1540
  561.5 76.6 %copy-start.16 = (f32[128]{0:T(128)S(1)}, f32[128]{0:T(128)}, u32[]{:S(2)}) copy-start(f32[128]{0:T(128)} %param.25) | copy-start | bytes 1540
  562.0 1.4 collective-permute-start.3
  563.4 5.9 collective-permute-start.4
  569.3 6.6 %collective-permute-start.5 = (f32[128,129]{1,0:T(8,128)S(1)}, f32[128,129]{1,0:T(8,128)S(1)}, u32[]{:S(2)}, u32[]{:S(2)}) collective-permute-start(f32[128,129]{1,0:T(8,128)S(1)} %add.145), channel_id=1, source_target_pairs={{0,64},{32,96},{64,0},{96,32},{1,65},{33,97},{65,1},{97,33},{2,66}... | collective-permute-start | bytes 198152 | tf_op jit(solution)/shard_map/ppermute | solution.py:28
  575.9 5.3 collective-permute-start.6
  581.2 6.8 %collective-permute-start.7 = (f32[128,129]{1,0:T(8,128)S(1)}, f32[128,129]{1,0:T(8,128)S(1)}, u32[]{:S(2)}, u32[]{:S(2)}) collective-permute-start(f32[128,129]{1,0:T(8,128)S(1)} %add.147), channel_id=1, source_target_pairs={{0,2},{1,3},{2,0},{3,1},{4,6},{5,7},{6,4},{7,5},{8,10},{9,11},{10,... | collective-permute-start | bytes 198152 | tf_op jit(solution)/shard_map/ppermute | solution.py:28
  587.9 6.2 collective-permute-start.8
  594.1 10.2 %collective-permute-start.9 = (f32[128,129]{1,0:T(8,128)S(1)}, f32[128,129]{1,0:T(8,128)S(1)}, u32[]{:S(2)}, u32[]{:S(2)}) collective-permute-start(f32[128,129]{1,0:T(8,128)S(1)} %add.149), channel_id=1, source_target_pairs={{0,8},{1,9},{2,10},{3,11},{4,12},{5,13},{6,14},{7,15},{8,0},{9,1},... | collective-permute-start | bytes 198152 | tf_op jit(solution)/shard_map/ppermute | solution.py:28
  604.3 10.4 %collective-permute-start.10 = (f32[128,129]{1,0:T(8,128)S(1)}, f32[128,129]{1,0:T(8,128)S(1)}, u32[]{:S(2)}, u32[]{:S(2)}) collective-permute-start(f32[128,129]{1,0:T(8,128)S(1)} %add.150), channel_id=1, source_target_pairs={{0,16},{1,17},{2,18},{3,19},{4,20},{5,21},{6,22},{7,23},{8,24},{9,... | collective-permute-start | bytes 198152 | tf_op jit(solution)/shard_map/ppermute | solution.py:28
  638.4 1.1 copy-start.15
Sparse Core Ops, SparseCore 0:
  10.6 100.8 all-gather.1

commit v2 on v1

--- a/solution.py
+++ b/solution.py
@@ -30,8 +30,38 @@
     return value
 
 
-def trsm(a, b, transpose=False):
-    return lax.linalg.triangular_solve(a, b, left_side=True, lower=True, transpose_a=transpose)
+BLOCK = 128
+
+
+def diagonal_inverses(lower):
+    blocks = lower.shape[0] // BLOCK
+    diag = jnp.stack([lower[i * BLOCK:(i + 1) * BLOCK, i * BLOCK:(i + 1) * BLOCK] for i in range(blocks)])
+    eye = jnp.broadcast_to(jnp.eye(BLOCK, dtype=lower.dtype), diag.shape)
+    return lax.linalg.triangular_solve(diag, eye, left_side=True, lower=True)
+
+
+def forward_solve(lower, inverses, rhs):
+    parts = []
+    for i in range(inverses.shape[0]):
+        rows = slice(i * BLOCK, (i + 1) * BLOCK)
+        acc = rhs[rows]
+        if i:
+            acc = acc - jnp.dot(lower[rows, : i * BLOCK], jnp.concatenate(parts, axis=0), precision=highest)
+        parts.append(jnp.dot(inverses[i], acc, precision=highest))
+    return jnp.concatenate(parts, axis=0)
+
+
+def backward_solve(lower, inverses, rhs):
+    count = inverses.shape[0]
+    parts = [None] * count
+    for i in reversed(range(count)):
+        rows = slice(i * BLOCK, (i + 1) * BLOCK)
+        acc = rhs[rows]
+        if i < count - 1:
+            later = jnp.concatenate(parts[i + 1:], axis=0)
+            acc = acc - jnp.dot(lower[(i + 1) * BLOCK:, rows].T, later, precision=highest)
+        parts[i] = jnp.dot(inverses[i].T, acc, precision=highest)
+    return jnp.concatenate(parts, axis=0)
 
 
 def on_device(
@@ -71,7 +101,8 @@
     h_nr = hessian[count:, :count]
     h_rr = hessian[:count, :count]
     l_nn = lax.linalg.cholesky(h_nn)
-    solved = trsm(l_nn, jnp.concatenate([h_nr, rhs[count:]], axis=1))
+    inv_nn = diagonal_inverses(l_nn)
+    solved = forward_solve(l_nn, inv_nn, jnp.concatenate([h_nr, rhs[count:]], axis=1))
     x_nr = solved[:, :count]
     y_n = solved[:, count:]
     schur = h_rr - jnp.dot(x_nr.T, x_nr, precision=highest)
@@ -91,11 +122,14 @@
         axis=0,
     )
     lower = lax.linalg.cholesky(system)
-    ramp_both = jax.scipy.linalg.cho_solve(
-        (lower, True), jnp.concatenate([part0[:, count:], part1[:, count:]], axis=0)
+    inv_sys = diagonal_inverses(lower)
+    ramp_both = backward_solve(
+        lower,
+        inv_sys,
+        forward_solve(lower, inv_sys, jnp.concatenate([part0[:, count:], part1[:, count:]], axis=0)),
     )
     x_r = jnp.where(first, ramp_both[:count], ramp_both[count:])
-    x_n = trsm(l_nn, y_n - jnp.dot(x_nr, x_r, precision=highest), transpose=True)
+    x_n = backward_solve(l_nn, inv_nn, y_n - jnp.dot(x_nr, x_r, precision=highest))
     solution_cols = jnp.concatenate([x_r, x_n], axis=0)
     step_vec = solution_cols[:, 0]
     step_cols = solution_cols[:, 1:]

time: 653 us -> 614 us (0.940)
  local copies, waits for them, and re-layouts: 60.2 us -> 28.9 us
    another operation x33 -> x2, local copies, waits for them, and re-layouts: 34.9 us -> 0.02 us  [diagonal_inverses(): jnp.stack([lower[i * BLOCK:(i + 1) * BLOCK, i * BLOCK:(i + 1) * BLOCK] fo...]
    another operation x36 -> x2, matrix products: 33.1 us -> 1.38 us  [diagonal_inverses(): return lax.linalg.triangular_solve(diag, eye, left_side=True, lower=True)]
    dot_general x0 -> x36, matrix products: none -> 28.5 us  [the longest x8 11 us: forward_solve(): jnp.dot(lower[rows, :i * BLOCK], jnp.concatenate(parts, axis=0), precisio...]
    another operation x6 -> x5, other arithmetic: 105 us -> 98.3 us  [diagonal_inverses(): return lax.linalg.triangular_solve(diag, eye, left_side=True, lower=True)]
where the time goes in v2:
time: 614 us; the launch traced here: 608 us
  other arithmetic  338 us (55%)
  waiting for transfers between devices  146 us (24%)
  matrix products  61.8 us (10%)
  local copies, waits for them, and re-layouts  28.9 us (5%)
  between operations  21.8 us (4%)
  starting transfers between devices  11.3 us (2%)
    another operation x22, other arithmetic, on_device(): l_nn = lax.linalg.cholesky(h_nn)  127 us
    all_gather x1, waiting for transfers between devices, on_device(): half = lax.all_gather(mine_half, 'line', axis=0, tiled=True)  101 us
    another operation x5, other arithmetic, diagonal_inverses(): return lax.linalg.triangular_solve(diag, eye, left_side=True, lower=True)  98.3 us
    another operation x15, other arithmetic, on_device(): lower = lax.linalg.cholesky(system)  79.7 us
    ppermute x8, waiting for transfers between devices, butterfly_sum(): value = value + lax.ppermute(value, axis, pairs)  41.9 us
    another operation x10, matrix products, on_device(): l_nn = lax.linalg.cholesky(h_nn)  15.6 us
    another operation x3, other arithmetic, on_device(): link_lower = jnp.linalg.cholesky(link_system)  12.4 us
  transfers between devices with their start and end apart: 12, of which 11 were waited for; matrix products, arithmetic and copies ran while one was open for 1% of the time, Pallas kernels for 0%

profile of v2, /device:TPU:2, one launch (start us, length us, event | category | flops | bytes accessed | tf_op | source)
XLA Modules:
  0.0 607.9 jit_solution(14177595898608028591)
XLA Ops:
  9.1 1.3 collective-permute-done
  10.4 101.1 %all-gather.2.cloned.1.call-done = bf16[32,128,1024]{2,1,0:T(8,128)(2,1)} async-done(((bf16[1,128,1024]{2,1,0:T(8,128)(2,1)}), bf16[32,128,1024]{2,1,0:T(8,128)(2,1)}) %all-gather.2.cloned.1.call-update) | async-done | bytes 8388624 | tf_op jit(solution)/shard_map/all_gather | solution.py:87
  111.4 5.4 gather_fusion.1
  116.9 3.3 broadcast_select_fusion
  120.5 5.4 gather_fusion
  125.9 6.2 %bitcast_add_fusion = f32[1024,1024]{0,1:T(8,128)S(1)} fusion(f32[1024]{0:T(1024)S(1)} %pad_add_fusion, bf16[8,128,1024]{2,1,0:T(8,128)(2,1)} %collective-permute-done.1, bf16[8,128,1024]{2,1,0:T(8,128)(2,1)} %gather_fusion, f32[8,128]{1,0:T(8,128)S(1)} %bitcast.235, pred[8]{0:T(512)(128)(4,1)S(1)} %get-tuple-element.4, pred[8]{0:T(512)(128)(4,1)S(1)} %get-tuple-element.52), kind=kOutput, calls=%fused_computation.2 | convolution fusion | flops 2157969408 | bytes 8396816 | tf_op jit(solution)/shard_map/dot_general | solution.py:14
  132.2 1.8 slice.425
  134.9 3.3 copy.62
  138.2 2.7 fusion.1
  140.9 1.4 copy-done.3
  142.4 11.7 %cholesky.207 = f32[128,128]{1,0:T(8,128)S(1)} custom-call(f32[128,128]{1,0:T(8,128)S(1)} %copy.63), custom_call_target="Cholesky" | custom-call | tf_op jit(solution)/shard_map/cholesky | solution.py:103
  154.1 9.8 %custom-call.53 = f32[1,128,128]{1,2,0:T(8,128)S(1)} custom-call(f32[1,128,128]{2,1,0:T(8,128)S(1)} %get-tuple-element.51), custom_call_target="InvertDiagBlocksLowerTriangular" | custom-call | tf_op jit(solution)/shard_map/cholesky | solution.py:103
  164.0 1.6 cholesky.234
  165.6 2.4 constant_dynamic-update-slice_fusion.26
  168.0 1.4 slice_subtract_fusion
  169.6 11.7 %cholesky.227 = f32[128,128]{1,0:T(8,128)S(1)} custom-call(f32[128,128]{1,0:T(8,128)S(1)} %copy.65), custom_call_target="Cholesky" | custom-call | tf_op jit(solution)/shard_map/cholesky | solution.py:103
  181.9 10.2 %custom-call.54 = f32[1,128,128]{1,2,0:T(8,128)S(1)} custom-call(f32[1,128,128]{2,1,0:T(8,128)S(1)} %get-tuple-element.48), custom_call_target="InvertDiagBlocksLowerTriangular" | custom-call | tf_op jit(solution)/shard_map/cholesky | solution.py:103
  192.1 1.3 convolution_dynamic-update-slice_fusion
  193.4 1.9 slice_subtract_fusion.1
  195.4 11.7 %cholesky.252 = f32[128,128]{1,0:T(8,128)S(1)} custom-call(f32[128,128]{1,0:T(8,128)S(1)} %copy.67), custom_call_target="Cholesky" | custom-call | tf_op jit(solution)/shard_map/cholesky | solution.py:103
  208.4 9.8 %custom-call.61 = f32[1,128,128]{1,2,0:T(8,128)S(1)} custom-call(f32[1,128,128]{2,1,0:T(8,128)S(1)} %get-tuple-element.45), custom_call_target="InvertDiagBlocksLowerTriangular" | custom-call | tf_op jit(solution)/shard_map/cholesky/custom-call.15 | solution.py:103
  219.5 1.9 slice_subtract_fusion.3
  221.5 11.9 %cholesky.449 = f32[128,128]{1,0:T(8,128)S(1)} custom-call(f32[128,128]{1,0:T(8,128)S(1)} %copy.70), custom_call_target="Cholesky" | custom-call | tf_op jit(solution)/shard_map/cholesky | solution.py:103
  234.7 9.8 %custom-call.62 = f32[1,128,128]{1,2,0:T(8,128)S(1)} custom-call(f32[1,128,128]{2,1,0:T(8,128)S(1)} %get-tuple-element.42), custom_call_target="InvertDiagBlocksLowerTriangular" | custom-call | tf_op jit(solution)/shard_map/cholesky/custom-call.16 | solution.py:103
  245.6 1.8 slice_subtract_fusion.4
  247.6 11.7 %cholesky.464 = f32[128,128]{1,0:T(8,128)S(1)} custom-call(f32[128,128]{1,0:T(8,128)S(1)} %copy.73), custom_call_target="Cholesky" | custom-call | tf_op jit(solution)/shard_map/cholesky | solution.py:103
  260.6 9.8 %custom-call.63 = f32[1,128,128]{1,2,0:T(8,128)S(1)} custom-call(f32[1,128,128]{2,1,0:T(8,128)S(1)} %get-tuple-element.39), custom_call_target="InvertDiagBlocksLowerTriangular" | custom-call | tf_op jit(solution)/shard_map/cholesky/custom-call.17 | solution.py:103
  271.3 1.5 slice_subtract_fusion.11
  273.0 12.1 %cholesky.478 = f32[128,128]{1,0:T(8,128)S(1)} custom-call(f32[128,128]{1,0:T(8,128)S(1)} %copy.76), custom_call_target="Cholesky" | custom-call | tf_op jit(solution)/shard_map/cholesky | solution.py:103
  290.8 1.8 select_select_fusion
  292.7 1.3 copy-done.1
  294.1 59.0 %custom-call.55 = f32[6,1,128,128]{2,3,1,0:T(8,128)S(1)} custom-call(f32[6,1,128,128]{3,2,1,0:T(8,128)S(1)} %broadcast_select_fusion.3), custom_call_target="InvertDiagBlocksLowerTriangular" | custom-call | tf_op jit(solution)/shard_map/triangular_solve | solution.py:40
  354.3 1.3 fusion.151
  356.2 1.4 fusion.39
  358.1 1.7 fusion.24
  360.3 1.8 fusion.12
  362.5 2.1 fusion.47
  365.1 1.8 slice_subtract_fusion.2
  368.7 1.3 collective-permute-done.2
  371.8 1.3 copy.79
  373.1 1.5 fusion.10
  375.6 11.7 %cholesky.492 = f32[128,128]{1,0:T(8,128)S(1)} custom-call(f32[128,128]{1,0:T(8,128)S(1)} %cholesky.576), custom_call_target="Cholesky" | custom-call | tf_op jit(solution)/shard_map/cholesky | solution.py:124
  387.5 9.8 %custom-call.64 = f32[1,128,128]{1,2,0:T(8,128)S(1)} custom-call(f32[1,128,128]{2,1,0:T(8,128)S(1)} %get-tuple-element.35), custom_call_target="InvertDiagBlocksLowerTriangular" | custom-call | tf_op jit(solution)/shard_map/cholesky/custom-call.15 | solution.py:124
  399.8 11.7 %cholesky.503 = f32[128,128]{1,0:T(8,128)S(1)} custom-call(f32[128,128]{1,0:T(8,128)S(1)} %cholesky.580), custom_call_target="Cholesky" | custom-call | tf_op jit(solution)/shard_map/cholesky | solution.py:124
  412.8 10.0 %custom-call.65 = f32[1,128,128]{1,2,0:T(8,128)S(1)} custom-call(f32[1,128,128]{2,1,0:T(8,128)S(1)} %get-tuple-element.32), custom_call_target="InvertDiagBlocksLowerTriangular" | custom-call | tf_op jit(solution)/shard_map/cholesky/custom-call.16 | solution.py:124
  424.4 11.7 %cholesky.520 = f32[128,128]{1,0:T(8,128)S(1)} custom-call(f32[128,128]{1,0:T(8,128)S(1)} %cholesky.585), custom_call_target="Cholesky" | custom-call | tf_op jit(solution)/shard_map/cholesky | solution.py:124
  436.8 9.8 %custom-call.66 = f32[1,128,128]{1,2,0:T(8,128)S(1)} custom-call(f32[1,128,128]{2,1,0:T(8,128)S(1)} %get-tuple-element.29), custom_call_target="InvertDiagBlocksLowerTriangular" | custom-call | tf_op jit(solution)/shard_map/cholesky/custom-call.17 | solution.py:124
  448.1 12.1 %cholesky.533 = f32[128,128]{1,0:T(8,128)S(1)} custom-call(f32[128,128]{1,0:T(8,128)S(1)} %convolution_subtract_fusion.12), custom_call_target="Cholesky" | custom-call | tf_op jit(solution)/shard_map/cholesky | solution.py:124
  464.8 39.3 %custom-call.56 = f32[4,1,128,128]{2,3,1,0:T(8,128)S(1)} custom-call(f32[4,1,128,128]{3,2,1,0:T(8,128)S(1)} %maximum_select_fusion), custom_call_target="InvertDiagBlocksLowerTriangular" | custom-call | tf_op jit(solution)/shard_map/triangular_solve | solution.py:40
  518.0 1.3 convolution_subtract_fusion.10
  519.6 1.3 convolution_subtract_fusion.9
  521.2 1.5 convolution_subtract_fusion.4
  525.7 5.2 collective-permute-done.4
  530.9 2.2 collective-permute-start.5
  533.1 4.4 collective-permute-done.5
  538.0 5.2 collective-permute-done.6
  544.3 5.4 collective-permute-done.7
  549.8 5.6 collective-permute-done.8
  555.5 1.8 collective-permute-start.9
  557.3 8.4 %collective-permute-done.9 = f32[128,129]{1,0:T(8,128)S(1)} collective-permute-done((f32[128,129]{1,0:T(8,128)S(1)}, f32[128,129]{1,0:T(8,128)S(1)}, u32[]{:S(2)}, u32[]{:S(2)}) %collective-permute-start.9) | collective-permute-done | bytes 66080 | tf_op jit(solution)/shard_map/ppermute | solution.py:28
  565.7 3.7 collective-permute-start.10
  569.4 6.7 %collective-permute-done.10 = f32[128,129]{1,0:T(8,128)S(1)} collective-permute-done((f32[128,129]{1,0:T(8,128)S(1)}, f32[128,129]{1,0:T(8,128)S(1)}, u32[]{:S(2)}, u32[]{:S(2)}) %collective-permute-start.10) | collective-permute-done | bytes 66080 | tf_op jit(solution)/shard_map/ppermute | solution.py:28
  576.5 11.7 %cholesky.544 = f32[128,128]{1,0:T(8,128)S(1)} custom-call(f32[128,128]{1,0:T(8,128)S(1)} %fusion.167), custom_call_target="Cholesky" | custom-call | tf_op jit(solution)/shard_map/jit(cholesky)/cholesky | solution.py:144
  589.6 9.8 %custom-call.57 = f32[1,128,128]{1,2,0:T(8,128)S(1)} custom-call(f32[1,128,128]{2,1,0:T(8,128)S(1)} %fusion.142), custom_call_target="InvertDiagBlocksLowerTriangular" | custom-call | tf_op jit(solution)/shard_map/jit(_cho_solve)/triangular_solve | solution.py:145
  (189 shorter events, 53.4 us)
Async XLA Ops:
  7.2 1.0 copy-start
  7.2 104.3 %all-gather.2.cloned.1.call-start = ((), (), s32[]{:S(2)}) async-start(), calls=%async_computation | async-start | bytes 8650752 | tf_op jit(solution)/shard_map/all_gather | solution.py:87
  9.0 1.4 collective-permute-start
  116.9 3.3 copy-start.12
  116.9 3.4 copy-start.20
  116.9 3.6 copy-start.14
  116.9 3.6 copy-start.15
  116.9 3.7 copy-start.16
  120.1 5.8 collective-permute-start.1
  120.4 5.5 copy-start.21
  132.2 2.6 copy-start.2
  140.9 1.4 copy-start.3
  292.6 1.4 copy-start.1
  353.8 10.8 %copy-start.6 = (f32[6,128,128]{2,1,0:T(8,128)}, f32[6,128,128]{2,1,0:T(8,128)S(1)}, u32[]{:S(2)}) copy-start(f32[6,128,128]{2,1,0:T(8,128)S(1)} %fusion.43) | copy-start | bytes 1179652
  367.9 2.1 collective-permute-start.2
  370.1 0.8 copy-start.10
  370.1 0.9 copy-start.11
  371.0 0.7 copy-start.9
  374.6 1.0 copy-start.8
  463.8 1.0 copy-start.4
  464.8 45.8 %copy-start.5 = (f32[512,512]{1,0:T(8,128)S(1)}, f32[512,512]{1,0:T(8,128)}, u32[]{:S(2)}) copy-start(f32[512,512]{1,0:T(8,128)} %copy-done.4) | copy-start | bytes 3145732
  510.6 4.3 copy-start.7
  516.2 6.8 %copy-start.13 = (bf16[1,1,1024,128]{3,2,1,0:T(8,128)(2,1)S(1)}, bf16[1,1,1024,128]{3,2,1,0:T(8,128)(2,1)}, u32[]{:S(2)}) copy-start(bf16[1,1,1024,128]{3,2,1,0:T(8,128)(2,1)} %param.22) | copy-start | bytes 786436
  523.0 53.2 %copy-start.17 = (f32[128]{0:T(128)S(1)}, f32[128]{0:T(128)}, u32[]{:S(2)}) copy-start(f32[128]{0:T(128)} %param.24) | copy-start | bytes 1540
  523.1 76.3 %copy-start.19 = (f32[128]{0:T(128)S(1)}, f32[128]{0:T(128)}, u32[]{:S(2)}) copy-start(f32[128]{0:T(128)} %param.25) | copy-start | bytes 1540
  523.6 1.5 collective-permute-start.3
  525.0 5.9 collective-permute-start.4
  530.9 6.6 %collective-permute-start.5 = (f32[128,129]{1,0:T(8,128)S(1)}, f32[128,129]{1,0:T(8,128)S(1)}, u32[]{:S(2)}, u32[]{:S(2)}) collective-permute-start(f32[128,129]{1,0:T(8,128)S(1)} %add.139), channel_id=1, source_target_pairs={{0,64},{32,96},{64,0},{96,32},{1,65},{33,97},{65,1},{97,33},{2,66}... | collective-permute-start | bytes 198152 | tf_op jit(solution)/shard_map/ppermute | solution.py:28
  537.5 5.6 collective-permute-start.6
  543.2 6.6 %collective-permute-start.7 = (f32[128,129]{1,0:T(8,128)S(1)}, f32[128,129]{1,0:T(8,128)S(1)}, u32[]{:S(2)}, u32[]{:S(2)}) collective-permute-start(f32[128,129]{1,0:T(8,128)S(1)} %add.141), channel_id=1, source_target_pairs={{0,2},{1,3},{2,0},{3,1},{4,6},{5,7},{6,4},{7,5},{8,10},{9,11},{10,... | collective-permute-start | bytes 198152 | tf_op jit(solution)/shard_map/ppermute | solution.py:28
  549.7 5.7 collective-permute-start.8
  555.5 10.2 %collective-permute-start.9 = (f32[128,129]{1,0:T(8,128)S(1)}, f32[128,129]{1,0:T(8,128)S(1)}, u32[]{:S(2)}, u32[]{:S(2)}) collective-permute-start(f32[128,129]{1,0:T(8,128)S(1)} %add.143), channel_id=1, source_target_pairs={{0,8},{1,9},{2,10},{3,11},{4,12},{5,13},{6,14},{7,15},{8,0},{9,1},... | collective-permute-start | bytes 198152 | tf_op jit(solution)/shard_map/ppermute | solution.py:28
  565.7 10.4 %collective-permute-start.10 = (f32[128,129]{1,0:T(8,128)S(1)}, f32[128,129]{1,0:T(8,128)S(1)}, u32[]{:S(2)}, u32[]{:S(2)}) collective-permute-start(f32[128,129]{1,0:T(8,128)S(1)} %add.144), channel_id=1, source_target_pairs={{0,16},{1,17},{2,18},{3,19},{4,20},{5,21},{6,22},{7,23},{8,24},{9,... | collective-permute-start | bytes 198152 | tf_op jit(solution)/shard_map/ppermute | solution.py:28
  599.8 1.1 copy-start.18
Sparse Core Ops, SparseCore 0:
  10.6 100.8 all-gather.1

commit v3 on v2

--- a/solution.py
+++ b/solution.py
@@ -36,8 +36,19 @@
 def diagonal_inverses(lower):
     blocks = lower.shape[0] // BLOCK
     diag = jnp.stack([lower[i * BLOCK:(i + 1) * BLOCK, i * BLOCK:(i + 1) * BLOCK] for i in range(blocks)])
-    eye = jnp.broadcast_to(jnp.eye(BLOCK, dtype=lower.dtype), diag.shape)
-    return lax.linalg.triangular_solve(diag, eye, left_side=True, lower=True)
+    row = lax.broadcasted_iota(jnp.int32, (BLOCK, BLOCK), 0)
+    col = lax.broadcasted_iota(jnp.int32, (BLOCK, BLOCK), 1)
+    eye = (row == col).astype(lower.dtype)
+    inverse = eye / jnp.sum(diag * eye, axis=-1, keepdims=True)
+    size = 1
+    while size < BLOCK:
+        below = (row // (2 * size) == col // (2 * size)) & ((row // size) % 2 == 1) & ((col // size) % 2 == 0)
+        off = jnp.where(below, diag, 0.0)
+        inverse = inverse - jnp.matmul(
+            jnp.matmul(inverse, off, precision=highest), inverse, precision=highest
+        )
+        size *= 2
+    return inverse
 
 
 def forward_solve(lower, inverses, rhs):

time: 614 us -> 526 us (0.86)
  other arithmetic: 338 us -> 247 us
    another operation x5 -> x0, other arithmetic: 98.3 us -> none  [diagonal_inverses(): return lax.linalg.triangular_solve(diag, eye, left_side=True, lower=True)]
    dot_general x0 -> x28, matrix products: none -> 13.2 us  [the longest x14 6.71 us: diagonal_inverses(): jnp.matmul(jnp.matmul(inverse, off, precision=highest), inverse, precisio...]
    another operation x22, other arithmetic: 127 us -> 134 us  [on_device(): l_nn = lax.linalg.cholesky(h_nn)]
where the time goes in v3:
time: 526 us; the launch traced here: 520 us
  other arithmetic  247 us (47%)
  waiting for transfers between devices  146 us (28%)
  matrix products  65.3 us (12%)
  local copies, waits for them, and re-layouts  28.2 us (5%)
  between operations  22.7 us (4%)
  starting transfers between devices  11.1 us (2%)
    another operation x22, other arithmetic, on_device(): l_nn = lax.linalg.cholesky(h_nn)  134 us
    all_gather x1, waiting for transfers between devices, on_device(): half = lax.all_gather(mine_half, 'line', axis=0, tiled=True)  101 us
    another operation x15, other arithmetic, on_device(): lower = lax.linalg.cholesky(system)  79.4 us
    ppermute x8, waiting for transfers between devices, butterfly_sum(): value = value + lax.ppermute(value, axis, pairs)  42.2 us
    another operation x10, matrix products, on_device(): l_nn = lax.linalg.cholesky(h_nn)  12.5 us
    another operation x3, other arithmetic, on_device(): link_lower = jnp.linalg.cholesky(link_system)  12.4 us
  transfers between devices with their start and end apart: 12, of which 11 were waited for; matrix products, arithmetic and copies ran while one was open for 1% of the time, Pallas kernels for 0%

profile of v3, /device:TPU:2, one launch (start us, length us, event | category | flops | bytes accessed | tf_op | source)
XLA Modules:
  0.0 520.0 jit_solution(9849638358074395630)
XLA Ops:
  9.2 1.2 collective-permute-done
  10.4 101.1 %all-gather.2.cloned.1.call-done = bf16[32,128,1024]{2,1,0:T(8,128)(2,1)} async-done(((bf16[1,128,1024]{2,1,0:T(8,128)(2,1)}), bf16[32,128,1024]{2,1,0:T(8,128)(2,1)}) %all-gather.2.cloned.1.call-update) | async-done | bytes 8388624 | tf_op jit(solution)/shard_map/all_gather | solution.py:98
  111.4 4.1 gather_fusion.1
  115.6 1.6 broadcast_select_fusion
  121.0 4.1 gather_fusion
  125.1 6.9 %bitcast_add_fusion = f32[1024,1024]{0,1:T(8,128)} fusion(f32[1024]{0:T(1024)S(1)} %pad_add_fusion, bf16[8,128,1024]{2,1,0:T(8,128)(2,1)} %collective-permute-done.1, bf16[8,128,1024]{2,1,0:T(8,128)(2,1)S(1)} %gather_fusion, f32[8,128]{1,0:T(8,128)S(1)} %bitcast.265, pred[8]{0:T(512)(128)(4,1)S(1)} %get-tuple-element.4, pred[8]{0:T(512)(128)(4,1)S(1)} %get-tuple-element.59), kind=kOutput, calls=%fused_computation.2 | convolution fusion | flops 2157969408 | bytes 8396816 | tf_op jit(solution)/shard_map/dot_general | solution.py:14
  132.0 3.2 slice.417
  135.2 2.2 copy.62
  137.4 3.4 fusion.1
  141.8 11.7 %cholesky.200 = f32[128,128]{1,0:T(8,128)S(1)} custom-call(f32[128,128]{1,0:T(8,128)S(1)} %copy.63), custom_call_target="Cholesky" | custom-call | tf_op jit(solution)/shard_map/cholesky | solution.py:114
  154.1 9.8 %custom-call.47 = f32[1,128,128]{1,2,0:T(8,128)S(1)} custom-call(f32[1,128,128]{2,1,0:T(8,128)S(1)} %get-tuple-element.51), custom_call_target="InvertDiagBlocksLowerTriangular" | custom-call | tf_op jit(solution)/shard_map/cholesky | solution.py:114
  163.9 1.4 fusion.65
  166.3 1.5 slice_subtract_fusion
  167.8 1.2 slice.425
  169.7 1.6 copy.65
  171.3 13.2 %cholesky.222 = f32[128,128]{1,0:T(8,128)} custom-call(f32[128,128]{1,0:T(8,128)} %copy.65), custom_call_target="Cholesky" | custom-call | tf_op jit(solution)/shard_map/cholesky | solution.py:114
  185.5 2.0 select_reduce_fusion.9
  187.5 11.4 %custom-call.48 = f32[1,128,128]{1,2,0:T(8,128)} custom-call(f32[1,128,128]{2,1,0:T(8,128)} %get-tuple-element.48), custom_call_target="InvertDiagBlocksLowerTriangular" | custom-call | tf_op jit(solution)/shard_map/cholesky | solution.py:114
  198.9 1.4 convolution_dynamic-update-slice_fusion
  200.3 1.6 slice_subtract_fusion.1
  202.7 13.2 %cholesky.247 = f32[128,128]{1,0:T(8,128)} custom-call(f32[128,128]{1,0:T(8,128)} %copy.69), custom_call_target="Cholesky" | custom-call | tf_op jit(solution)/shard_map/cholesky | solution.py:114
  217.5 10.4 %custom-call.53 = f32[1,128,128]{1,2,0:T(8,128)} custom-call(f32[1,128,128]{2,1,0:T(8,128)S(1)} %get-tuple-element.45), custom_call_target="InvertDiagBlocksLowerTriangular" | custom-call | tf_op jit(solution)/shard_map/cholesky/custom-call.15 | solution.py:114
  227.9 1.3 fusion.5
  229.3 1.6 slice_subtract_fusion.3
  231.6 12.9 %cholesky.438 = f32[128,128]{1,0:T(8,128)S(1)} custom-call(f32[128,128]{1,0:T(8,128)} %copy.72), custom_call_target="Cholesky" | custom-call | tf_op jit(solution)/shard_map/cholesky | solution.py:114
  245.3 9.8 %custom-call.54 = f32[1,128,128]{1,2,0:T(8,128)S(1)} custom-call(f32[1,128,128]{2,1,0:T(8,128)S(1)} %get-tuple-element.42), custom_call_target="InvertDiagBlocksLowerTriangular" | custom-call | tf_op jit(solution)/shard_map/cholesky/custom-call.16 | solution.py:114
  255.5 1.6 slice_subtract_fusion.4
  257.2 11.7 %cholesky.453 = f32[128,128]{1,0:T(8,128)S(1)} custom-call(f32[128,128]{1,0:T(8,128)S(1)} %copy.75), custom_call_target="Cholesky" | custom-call | tf_op jit(solution)/shard_map/cholesky | solution.py:114
  269.7 9.8 %custom-call.55 = f32[1,128,128]{1,2,0:T(8,128)S(1)} custom-call(f32[1,128,128]{2,1,0:T(8,128)S(1)} %get-tuple-element.39), custom_call_target="InvertDiagBlocksLowerTriangular" | custom-call | tf_op jit(solution)/shard_map/cholesky/custom-call.17 | solution.py:114
  279.8 1.3 slice_subtract_fusion.11
  281.2 11.9 %cholesky.467 = f32[128,128]{1,0:T(8,128)S(1)} custom-call(f32[128,128]{1,0:T(8,128)S(1)} %copy.78), custom_call_target="Cholesky" | custom-call | tf_op jit(solution)/shard_map/cholesky | solution.py:114
  293.8 1.4 compare_reduce_fusion.9
  314.5 1.8 slice_subtract_fusion.2
  318.3 1.3 collective-permute-done.2
  320.7 1.3 copy.80
  322.0 1.4 fusion.10
  324.4 11.7 %cholesky.481 = f32[128,128]{1,0:T(8,128)S(1)} custom-call(f32[128,128]{1,0:T(8,128)S(1)} %cholesky.565), custom_call_target="Cholesky" | custom-call | tf_op jit(solution)/shard_map/cholesky | solution.py:135
  336.3 9.8 %custom-call.56 = f32[1,128,128]{1,2,0:T(8,128)S(1)} custom-call(f32[1,128,128]{2,1,0:T(8,128)S(1)} %get-tuple-element.35), custom_call_target="InvertDiagBlocksLowerTriangular" | custom-call | tf_op jit(solution)/shard_map/cholesky/custom-call.15 | solution.py:135
  346.1 1.2 constant_dynamic-update-slice_fusion.24
  347.3 1.3 convolution_subtract_fusion.15
  348.6 11.7 %cholesky.492 = f32[128,128]{1,0:T(8,128)S(1)} custom-call(f32[128,128]{1,0:T(8,128)S(1)} %cholesky.569), custom_call_target="Cholesky" | custom-call | tf_op jit(solution)/shard_map/cholesky | solution.py:135
  361.6 10.0 %custom-call.57 = f32[1,128,128]{1,2,0:T(8,128)S(1)} custom-call(f32[1,128,128]{2,1,0:T(8,128)S(1)} %get-tuple-element.32), custom_call_target="InvertDiagBlocksLowerTriangular" | custom-call | tf_op jit(solution)/shard_map/cholesky/custom-call.16 | solution.py:135
  371.9 1.3 convolution_subtract_fusion.17
  373.2 11.7 %cholesky.509 = f32[128,128]{1,0:T(8,128)S(1)} custom-call(f32[128,128]{1,0:T(8,128)S(1)} %cholesky.574), custom_call_target="Cholesky" | custom-call | tf_op jit(solution)/shard_map/cholesky | solution.py:135
  385.6 9.8 %custom-call.58 = f32[1,128,128]{1,2,0:T(8,128)S(1)} custom-call(f32[1,128,128]{2,1,0:T(8,128)S(1)} %get-tuple-element.29), custom_call_target="InvertDiagBlocksLowerTriangular" | custom-call | tf_op jit(solution)/shard_map/cholesky/custom-call.17 | solution.py:135
  395.6 1.2 convolution_subtract_fusion.26
  396.9 11.9 %cholesky.522 = f32[128,128]{1,0:T(8,128)S(1)} custom-call(f32[128,128]{1,0:T(8,128)S(1)} %convolution_subtract_fusion.26), custom_call_target="Cholesky" | custom-call | tf_op jit(solution)/shard_map/cholesky | solution.py:135
  418.3 1.2 fusion.202
  428.3 1.2 convolution_subtract_fusion.19
  429.8 1.3 convolution_subtract_fusion.24
  431.4 1.3 convolution_subtract_fusion.23
  433.1 1.5 convolution_subtract_fusion.18
  437.7 5.2 collective-permute-done.4
  443.0 2.2 collective-permute-start.5
  445.1 4.4 collective-permute-done.5
  449.9 5.2 collective-permute-done.6
  456.2 5.4 %collective-permute-done.7 = f32[128,129]{1,0:T(8,128)S(1)} collective-permute-done((f32[128,129]{1,0:T(8,128)S(1)}, f32[128,129]{1,0:T(8,128)S(1)}, u32[]{:S(2)}, u32[]{:S(2)}) %collective-permute-start.7) | collective-permute-done | bytes 66080 | tf_op jit(solution)/shard_map/ppermute | solution.py:28
  461.7 5.6 %collective-permute-done.8 = f32[128,129]{1,0:T(8,128)S(1)} collective-permute-done((f32[128,129]{1,0:T(8,128)S(1)}, f32[128,129]{1,0:T(8,128)S(1)}, u32[]{:S(2)}, u32[]{:S(2)}) %collective-permute-start.8) | collective-permute-done | bytes 66080 | tf_op jit(solution)/shard_map/ppermute | solution.py:28
  467.4 1.5 collective-permute-start.9
  468.9 8.7 %collective-permute-done.9 = f32[128,129]{1,0:T(8,128)S(1)} collective-permute-done((f32[128,129]{1,0:T(8,128)S(1)}, f32[128,129]{1,0:T(8,128)S(1)}, u32[]{:S(2)}, u32[]{:S(2)}) %collective-permute-start.9) | collective-permute-done | bytes 66080 | tf_op jit(solution)/shard_map/ppermute | solution.py:28
  477.6 3.7 collective-permute-start.10
  481.2 6.7 %collective-permute-done.10 = f32[128,129]{1,0:T(8,128)S(1)} collective-permute-done((f32[128,129]{1,0:T(8,128)S(1)}, f32[128,129]{1,0:T(8,128)S(1)}, u32[]{:S(2)}, u32[]{:S(2)}) %collective-permute-start.10) | collective-permute-done | bytes 66080 | tf_op jit(solution)/shard_map/ppermute | solution.py:28
  488.4 11.7 %cholesky.533 = f32[128,128]{1,0:T(8,128)S(1)} custom-call(f32[128,128]{1,0:T(8,128)S(1)} %fusion.255), custom_call_target="Cholesky" | custom-call | tf_op jit(solution)/shard_map/jit(cholesky)/cholesky | solution.py:155
  501.4 9.8 %custom-call.49 = f32[1,128,128]{1,2,0:T(8,128)S(1)} custom-call(f32[1,128,128]{2,1,0:T(8,128)S(1)} %fusion.204), custom_call_target="InvertDiagBlocksLowerTriangular" | custom-call | tf_op jit(solution)/shard_map/jit(_cho_solve)/triangular_solve | solution.py:156
  (249 shorter events, 61.9 us)
Async XLA Ops:
  7.2 1.1 copy-start
  7.2 104.3 %all-gather.2.cloned.1.call-start = ((), (), s32[]{:S(2)}) async-start(), calls=%async_computation | async-start | bytes 8650752 | tf_op jit(solution)/shard_map/all_gather | solution.py:98
  9.0 1.4 collective-permute-start
  115.5 1.7 copy-start.9
  115.5 1.9 copy-start.31
  115.5 2.8 copy-start.23
  115.6 3.6 copy-start.25
  115.6 3.6 copy-start.27
  117.2 7.9 %collective-permute-start.1 = (bf16[8,128,1024]{2,1,0:T(8,128)(2,1)}, bf16[8,128,1024]{2,1,0:T(8,128)(2,1)}, u32[]{:S(2)}, u32[]{:S(2)}) collective-permute-start(bf16[8,128,1024]{2,1,0:T(8,128)(2,1)} %broadcast_select_fusion), channel_id=1, source_target_pairs={{0,128},{128,0},{1,129},{129,1},{2,130},{130,2},{3,131},{131,3},{4... | collective-permute-start | bytes 6291464 | tf_op jit(solution)/shard_map/ppermute | solution.py:102
  117.5 0.8 copy-start.4
  119.1 6.0 %copy-start.32 = (f32[1,1,8,128]{3,2,1,0:T(8,128)S(1)}, f32[1,1,8,128]{3,2,1,0:T(8,128)}, u32[]{:S(2)}) copy-start(f32[1,1,8,128]{3,2,1,0:T(8,128)} %param.19) | copy-start | bytes 12292
  153.5 0.6 copy-start.11
  166.3 2.7 copy-start.12
  299.1 0.7 copy-start.21
  299.3 13.6 %copy-start.3 = (f32[768,768]{1,0:T(8,128)}, f32[768,768]{1,0:T(8,128)S(1)}, u32[]{:S(2)}) copy-start(f32[768,768]{1,0:T(8,128)S(1)} %select_select_fusion) | copy-start | bytes 7077892
  299.3 1.8 copy-start.19
  299.8 2.3 copy-start.17
  301.0 2.2 copy-start.15
  302.1 2.2 copy-start.14
  303.2 2.2 copy-start.13
  305.4 2.1 copy-start.2
  312.8 3.4 copy-start.5
  312.8 3.4 copy-start.24
  314.4 3.8 copy-start.26
  317.2 2.4 collective-permute-start.2
  319.6 0.8 copy-start.7
  319.7 0.9 copy-start.8
  323.4 1.0 copy-start.6
  371.8 40.6 %copy-start.22 = (pred[128,128]{1,0:T(8,128)(4,1)S(1)}, pred[128,128]{1,0:T(8,128)(4,1)}, u32[]{:S(2)}) copy-start(pred[128,128]{1,0:T(8,128)(4,1)} %get-tuple-element.58) | copy-start | bytes 49156
  412.1 1.3 copy-start.20
  412.3 2.0 copy-start.18
  412.9 2.1 copy-start.16
  428.0 7.1 %copy-start.10 = (bf16[1,1,1024,128]{3,2,1,0:T(8,128)(2,1)S(1)}, bf16[1,1,1024,128]{3,2,1,0:T(8,128)(2,1)}, u32[]{:S(2)}) copy-start(bf16[1,1,1024,128]{3,2,1,0:T(8,128)(2,1)} %param.22) | copy-start | bytes 786436
  435.1 53.0 %copy-start.28 = (f32[128]{0:T(128)S(1)}, f32[128]{0:T(128)}, u32[]{:S(2)}) copy-start(f32[128]{0:T(128)} %param.24) | copy-start | bytes 1540
  435.1 76.1 %copy-start.30 = (f32[128]{0:T(128)S(1)}, f32[128]{0:T(128)}, u32[]{:S(2)}) copy-start(f32[128]{0:T(128)} %param.25) | copy-start | bytes 1540
  435.2 77.5 %copy-start.1 = (bf16[2,128,1024]{2,1,0:T(8,128)(2,1)S(1)}, bf16[2,128,1024]{2,1,0:T(8,128)(2,1)}, u32[]{:S(2)}) copy-start(bf16[2,128,1024]{2,1,0:T(8,128)(2,1)} %param.17) | copy-start | bytes 1572868
  435.6 1.4 collective-permute-start.3
  437.1 5.8 %collective-permute-start.4 = (f32[128,129]{1,0:T(8,128)S(1)}, f32[128,129]{1,0:T(8,128)S(1)}, u32[]{:S(2)}, u32[]{:S(2)}) collective-permute-start(f32[128,129]{1,0:T(8,128)S(1)} %add.294), channel_id=1, source_target_pairs={{0,32},{32,0},{64,96},{96,64},{1,33},{33,1},{65,97},{97,65},{2,34}... | collective-permute-start | bytes 198152 | tf_op jit(solution)/shard_map/ppermute | solution.py:28
  443.0 6.6 %collective-permute-start.5 = (f32[128,129]{1,0:T(8,128)S(1)}, f32[128,129]{1,0:T(8,128)S(1)}, u32[]{:S(2)}, u32[]{:S(2)}) collective-permute-start(f32[128,129]{1,0:T(8,128)S(1)} %add.295), channel_id=1, source_target_pairs={{0,64},{32,96},{64,0},{96,32},{1,65},{33,97},{65,1},{97,33},{2,66}... | collective-permute-start | bytes 198152 | tf_op jit(solution)/shard_map/ppermute | solution.py:28
  449.5 5.5 %collective-permute-start.6 = (f32[128,129]{1,0:T(8,128)S(1)}, f32[128,129]{1,0:T(8,128)S(1)}, u32[]{:S(2)}, u32[]{:S(2)}) collective-permute-start(f32[128,129]{1,0:T(8,128)S(1)} %add.296), channel_id=1, source_target_pairs={{0,1},{1,0},{2,3},{3,2},{4,5},{5,4},{6,7},{7,6},{8,9},{9,8},{10,11... | collective-permute-start | bytes 198152 | tf_op jit(solution)/shard_map/ppermute | solution.py:28
  455.0 6.6 %collective-permute-start.7 = (f32[128,129]{1,0:T(8,128)S(1)}, f32[128,129]{1,0:T(8,128)S(1)}, u32[]{:S(2)}, u32[]{:S(2)}) collective-permute-start(f32[128,129]{1,0:T(8,128)S(1)} %add.297), channel_id=1, source_target_pairs={{0,2},{1,3},{2,0},{3,1},{4,6},{5,7},{6,4},{7,5},{8,10},{9,11},{10,... | collective-permute-start | bytes 198152 | tf_op jit(solution)/shard_map/ppermute | solution.py:28
  461.6 5.7 %collective-permute-start.8 = (f32[128,129]{1,0:T(8,128)S(1)}, f32[128,129]{1,0:T(8,128)S(1)}, u32[]{:S(2)}, u32[]{:S(2)}) collective-permute-start(f32[128,129]{1,0:T(8,128)S(1)} %add.298), channel_id=1, source_target_pairs={{0,4},{1,5},{2,6},{3,7},{4,0},{5,1},{6,2},{7,3},{8,12},{9,13},{10,... | collective-permute-start | bytes 198152 | tf_op jit(solution)/shard_map/ppermute | solution.py:28
  467.4 10.2 %collective-permute-start.9 = (f32[128,129]{1,0:T(8,128)S(1)}, f32[128,129]{1,0:T(8,128)S(1)}, u32[]{:S(2)}, u32[]{:S(2)}) collective-permute-start(f32[128,129]{1,0:T(8,128)S(1)} %add.299), channel_id=1, source_target_pairs={{0,8},{1,9},{2,10},{3,11},{4,12},{5,13},{6,14},{7,15},{8,0},{9,1},... | collective-permute-start | bytes 198152 | tf_op jit(solution)/shard_map/ppermute | solution.py:28
  477.6 10.4 %collective-permute-start.10 = (f32[128,129]{1,0:T(8,128)S(1)}, f32[128,129]{1,0:T(8,128)S(1)}, u32[]{:S(2)}, u32[]{:S(2)}) collective-permute-start(f32[128,129]{1,0:T(8,128)S(1)} %add.300), channel_id=1, source_target_pairs={{0,16},{1,17},{2,18},{3,19},{4,20},{5,21},{6,22},{7,23},{8,24},{9,... | collective-permute-start | bytes 198152 | tf_op jit(solution)/shard_map/ppermute | solution.py:28
  511.6 1.1 copy-start.29
Sparse Core Ops, SparseCore 0:
  10.6 100.8 all-gather.1

commit v4 on v3

--- a/solution.py
+++ b/solution.py
@@ -19,15 +19,33 @@
     return hessian + jnp.diag(barrier_row + extra)
 
 
-def butterfly_sum(value, axes):
-    for axis in axes:
-        size = lax.axis_size(axis)
-        step = 1
-        while step < size:
-            pairs = [(i, i ^ step) for i in range(size)]
-            value = value + lax.ppermute(value, axis, pairs)
-            step *= 2
-    return value
+def group_sum(value, axis, stride, size):
+    if size == 1:
+        return value
+    length = lax.axis_size(axis)
+    place = (lax.axis_index(axis) // stride) % size
+
+    def member(i, k):
+        return i - ((i // stride) % size) * stride + k * stride
+
+    received = [value]
+    for shift in range(1, size):
+        pairs = [(i, member(i, ((i // stride) % size + shift) % size)) for i in range(length)]
+        received.append(lax.ppermute(value, axis, pairs))
+    ordered = jnp.take(jnp.stack(received), (place - jnp.arange(size)) % size, axis=0)
+    total = ordered[0]
+    for k in range(1, size):
+        total = total + ordered[k]
+    return total
+
+
+def all_sum(value):
+    value = group_sum(value, "tm", 1, lax.axis_size("tm"))
+    value = group_sum(value, "scen", 1, lax.axis_size("scen"))
+    line = lax.axis_size("line")
+    inner = min(4, line)
+    value = group_sum(value, "line", 1, inner)
+    return group_sum(value, "line", inner, line // inner)
 
 
 BLOCK = 128
@@ -146,7 +164,7 @@
     step_cols = solution_cols[:, 1:]
 
     local = jnp.dot(link_float.T, solution_cols, precision=highest)
-    total = butterfly_sum(local, ("tm", "scen", "line"))
+    total = all_sum(local)
     vec_total = total[:, 0]
     mat_total = total[:, 1:]
     inverse_count = 1.0 / (shards * lax.axis_size("scen") * lax.axis_size("line"))

time: 526 us -> 517 us (0.983)
  waiting for transfers between devices: 146 us -> 115 us
  starting transfers between devices: 11.1 us -> 25.2 us
    ppermute x8 -> x14, waiting for transfers between devices: 42.2 us -> 12.2 us  [group_sum(): received.append(lax.ppermute(value, axis, pairs))]
    ppermute x8 -> x14, starting transfers between devices: 9.94 us -> 24.1 us  [group_sum(): received.append(lax.ppermute(value, axis, pairs))]
  transfers between devices with their start and end apart: 12 -> 18, of which waited for: 11 -> 11; matrix products, arithmetic and copies ran while one was open for 1% -> 2% of each run, Pallas kernels for 0% -> 0%
where the time goes in v4:
time: 517 us; the launch traced here: 509 us
  other arithmetic  250 us (48%)
  waiting for transfers between devices  115 us (22%)
  matrix products  65.3 us (13%)
  local copies, waits for them, and re-layouts  31.3 us (6%)
  starting transfers between devices  25.2 us (5%)
  between operations  22.6 us (4%)
    another operation x22, other arithmetic, on_device(): l_nn = lax.linalg.cholesky(h_nn)  133 us
    all_gather x1, waiting for transfers between devices, on_device(): half = lax.all_gather(mine_half, 'line', axis=0, tiled=True)  101 us
    another operation x15, other arithmetic, on_device(): lower = lax.linalg.cholesky(system)  79.3 us
    ppermute x14, starting transfers between devices, group_sum(): received.append(lax.ppermute(value, axis, pairs))  24.1 us
    another operation x10, matrix products, on_device(): l_nn = lax.linalg.cholesky(h_nn)  12.5 us
    another operation x3, other arithmetic, on_device(): link_lower = jnp.linalg.cholesky(link_system)  12.4 us
    ppermute x14, waiting for transfers between devices, group_sum(): received.append(lax.ppermute(value, axis, pairs))  12.2 us
    another operation x2, other arithmetic, on_device(): link_step = jax.scipy.linalg.cho_solve((link_lower, True), right_side)  10.5 us
  transfers between devices with their start and end apart: 18, of which 11 were waited for; matrix products, arithmetic and copies ran while one was open for 2% of the time, Pallas kernels for 0%

profile of v4, /device:TPU:2, one launch (start us, length us, event | category | flops | bytes accessed | tf_op | source)
XLA Modules:
  0.0 509.3 jit_solution(2998314933258718501)
XLA Ops:
  10.4 101.1 %all-gather.2.cloned.1.call-done = bf16[32,128,1024]{2,1,0:T(8,128)(2,1)} async-done(((bf16[1,128,1024]{2,1,0:T(8,128)(2,1)}), bf16[32,128,1024]{2,1,0:T(8,128)(2,1)}) %all-gather.2.cloned.1.call-update) | async-done | bytes 8388624 | tf_op jit(solution)/shard_map/all_gather | solution.py:116
  111.4 4.1 gather_fusion.3
  115.6 1.6 broadcast_select_fusion
  122.8 4.1 gather_fusion.2
  126.9 6.9 %bitcast_add_fusion = f32[1024,1024]{0,1:T(8,128)} fusion(f32[1024]{0:T(1024)S(1)} %pad_add_fusion, bf16[8,128,1024]{2,1,0:T(8,128)(2,1)} %collective-permute-done.1, bf16[8,128,1024]{2,1,0:T(8,128)(2,1)S(1)} %gather_fusion.2, f32[8,128]{1,0:T(8,128)S(1)} %bitcast.314, pred[8]{0:T(512)(128)(4,1)S(1)} %get-tuple-element.8, pred[8]{0:T(512)(128)(4,1)S(1)} %get-tuple-element.62), kind=kOutput, calls=%fused_computation.6 | convolution fusion | flops 2157969408 | bytes 8396816 | tf_op jit(solution)/shard_map/dot_general | solution.py:14
  133.8 3.3 slice.497
  137.1 2.2 copy.61
  139.3 3.4 fusion.1
  143.7 11.7 %cholesky.200 = f32[128,128]{1,0:T(8,128)S(1)} custom-call(f32[128,128]{1,0:T(8,128)S(1)} %copy.62), custom_call_target="Cholesky" | custom-call | tf_op jit(solution)/shard_map/cholesky | solution.py:132
  156.0 9.8 %custom-call.47 = f32[1,128,128]{1,2,0:T(8,128)S(1)} custom-call(f32[1,128,128]{2,1,0:T(8,128)S(1)} %get-tuple-element.54), custom_call_target="InvertDiagBlocksLowerTriangular" | custom-call | tf_op jit(solution)/shard_map/cholesky | solution.py:132
  165.8 1.4 fusion.65
  168.2 1.5 slice_subtract_fusion
  169.6 1.2 slice.505
  171.6 1.6 copy.64
  173.2 13.2 %cholesky.222 = f32[128,128]{1,0:T(8,128)} custom-call(f32[128,128]{1,0:T(8,128)} %copy.64), custom_call_target="Cholesky" | custom-call | tf_op jit(solution)/shard_map/cholesky | solution.py:132
  187.4 2.0 select_reduce_fusion.9
  189.4 11.4 %custom-call.48 = f32[1,128,128]{1,2,0:T(8,128)} custom-call(f32[1,128,128]{2,1,0:T(8,128)} %get-tuple-element.51), custom_call_target="InvertDiagBlocksLowerTriangular" | custom-call | tf_op jit(solution)/shard_map/cholesky | solution.py:132
  200.8 1.4 convolution_dynamic-update-slice_fusion
  202.3 1.6 slice_subtract_fusion.1
  204.6 13.2 %cholesky.247 = f32[128,128]{1,0:T(8,128)} custom-call(f32[128,128]{1,0:T(8,128)} %copy.68), custom_call_target="Cholesky" | custom-call | tf_op jit(solution)/shard_map/cholesky | solution.py:132
  219.4 10.4 %custom-call.53 = f32[1,128,128]{1,2,0:T(8,128)} custom-call(f32[1,128,128]{2,1,0:T(8,128)S(1)} %get-tuple-element.48), custom_call_target="InvertDiagBlocksLowerTriangular" | custom-call | tf_op jit(solution)/shard_map/cholesky/custom-call.15 | solution.py:132
  229.8 1.3 fusion.5
  231.1 1.6 slice_subtract_fusion.3
  233.5 12.9 %cholesky.438 = f32[128,128]{1,0:T(8,128)S(1)} custom-call(f32[128,128]{1,0:T(8,128)} %copy.71), custom_call_target="Cholesky" | custom-call | tf_op jit(solution)/shard_map/cholesky | solution.py:132
  247.2 9.8 %custom-call.54 = f32[1,128,128]{1,2,0:T(8,128)S(1)} custom-call(f32[1,128,128]{2,1,0:T(8,128)S(1)} %get-tuple-element.45), custom_call_target="InvertDiagBlocksLowerTriangular" | custom-call | tf_op jit(solution)/shard_map/cholesky/custom-call.16 | solution.py:132
  257.4 1.6 slice_subtract_fusion.4
  259.1 11.7 %cholesky.453 = f32[128,128]{1,0:T(8,128)S(1)} custom-call(f32[128,128]{1,0:T(8,128)S(1)} %copy.74), custom_call_target="Cholesky" | custom-call | tf_op jit(solution)/shard_map/cholesky | solution.py:132
  271.5 9.8 %custom-call.55 = f32[1,128,128]{1,2,0:T(8,128)S(1)} custom-call(f32[1,128,128]{2,1,0:T(8,128)S(1)} %get-tuple-element.42), custom_call_target="InvertDiagBlocksLowerTriangular" | custom-call | tf_op jit(solution)/shard_map/cholesky/custom-call.17 | solution.py:132
  281.6 1.3 slice_subtract_fusion.11
  283.0 11.9 %cholesky.467 = f32[128,128]{1,0:T(8,128)S(1)} custom-call(f32[128,128]{1,0:T(8,128)S(1)} %copy.77), custom_call_target="Cholesky" | custom-call | tf_op jit(solution)/shard_map/cholesky | solution.py:132
  295.6 1.4 compare_reduce_fusion.9
  316.2 1.8 slice_subtract_fusion.2
  320.1 1.3 collective-permute-done.2
  322.5 1.3 copy.79
  323.8 1.4 fusion.10
  326.2 11.7 %cholesky.481 = f32[128,128]{1,0:T(8,128)S(1)} custom-call(f32[128,128]{1,0:T(8,128)S(1)} %cholesky.565), custom_call_target="Cholesky" | custom-call | tf_op jit(solution)/shard_map/cholesky | solution.py:153
  338.0 9.8 %custom-call.56 = f32[1,128,128]{1,2,0:T(8,128)S(1)} custom-call(f32[1,128,128]{2,1,0:T(8,128)S(1)} %get-tuple-element.38), custom_call_target="InvertDiagBlocksLowerTriangular" | custom-call | tf_op jit(solution)/shard_map/cholesky/custom-call.15 | solution.py:153
  347.8 1.2 constant_dynamic-update-slice_fusion.38
  349.1 1.3 convolution_subtract_fusion.15
  350.4 11.7 %cholesky.492 = f32[128,128]{1,0:T(8,128)S(1)} custom-call(f32[128,128]{1,0:T(8,128)S(1)} %cholesky.569), custom_call_target="Cholesky" | custom-call | tf_op jit(solution)/shard_map/cholesky | solution.py:153
  363.5 9.9 %custom-call.57 = f32[1,128,128]{1,2,0:T(8,128)S(1)} custom-call(f32[1,128,128]{2,1,0:T(8,128)S(1)} %get-tuple-element.35), custom_call_target="InvertDiagBlocksLowerTriangular" | custom-call | tf_op jit(solution)/shard_map/cholesky/custom-call.16 | solution.py:153
  373.7 1.3 convolution_subtract_fusion.17
  375.0 11.7 %cholesky.509 = f32[128,128]{1,0:T(8,128)S(1)} custom-call(f32[128,128]{1,0:T(8,128)S(1)} %cholesky.574), custom_call_target="Cholesky" | custom-call | tf_op jit(solution)/shard_map/cholesky | solution.py:153
  387.4 9.8 %custom-call.58 = f32[1,128,128]{1,2,0:T(8,128)S(1)} custom-call(f32[1,128,128]{2,1,0:T(8,128)S(1)} %get-tuple-element.32), custom_call_target="InvertDiagBlocksLowerTriangular" | custom-call | tf_op jit(solution)/shard_map/cholesky/custom-call.17 | solution.py:153
  397.4 1.2 convolution_subtract_fusion.26
  398.7 11.8 %cholesky.522 = f32[128,128]{1,0:T(8,128)S(1)} custom-call(f32[128,128]{1,0:T(8,128)S(1)} %convolution_subtract_fusion.26), custom_call_target="Cholesky" | custom-call | tf_op jit(solution)/shard_map/cholesky | solution.py:153
  431.4 1.3 convolution_subtract_fusion.24
  433.0 1.3 convolution_subtract_fusion.23
  434.7 1.5 convolution_subtract_fusion.18
  439.5 1.5 collective-permute-start.4
  442.2 2.1 collective-permute-start.6
  444.3 3.1 collective-permute-done.5
  448.7 2.1 collective-permute-start.8
  450.8 1.8 collective-permute-start.9
  452.6 2.2 collective-permute-done.7
  456.6 3.6 collective-permute-start.11
  460.2 1.6 collective-permute-start.12
  461.8 2.9 collective-permute-start.13
  464.7 2.2 collective-permute-start.14
  466.9 3.4 collective-permute-start.15
  471.3 3.2 collective-permute-done.14
  474.5 1.3 collective-permute-done.15
  478.0 11.7 %cholesky.533 = f32[128,128]{1,0:T(8,128)S(1)} custom-call(f32[128,128]{1,0:T(8,128)S(1)} %fusion.251), custom_call_target="Cholesky" | custom-call | tf_op jit(solution)/shard_map/jit(cholesky)/cholesky | solution.py:173
  491.0 9.8 %custom-call.49 = f32[1,128,128]{1,2,0:T(8,128)S(1)} custom-call(f32[1,128,128]{2,1,0:T(8,128)S(1)} %fusion.206), custom_call_target="InvertDiagBlocksLowerTriangular" | custom-call | tf_op jit(solution)/shard_map/jit(_cho_solve)/triangular_solve | solution.py:174
  (293 shorter events, 72.4 us)
Async XLA Ops:
  7.2 1.1 copy-start
  7.2 104.3 %all-gather.2.cloned.1.call-start = ((), (), s32[]{:S(2)}) async-start(), calls=%async_computation | async-start | bytes 8650752 | tf_op jit(solution)/shard_map/all_gather | solution.py:116
  9.0 1.4 collective-permute-start
  115.5 1.7 copy-start.9
  115.5 1.9 copy-start.33
  115.5 4.6 copy-start.23
  115.6 5.4 %copy-start.25 = (f32[256]{0:T(256)S(1)}, f32[256]{0:T(256)}, u32[]{:S(2)}) copy-start(f32[256]{0:T(256)} %param.25) | copy-start | bytes 3076
  115.6 5.4 %copy-start.27 = (f32[1,1,1024]{2,1,0:T(1,128)S(1)}, f32[1,1,1024]{2,1,0:T(1,128)}, u32[]{:S(2)}) copy-start(f32[1,1,1024]{2,1,0:T(1,128)} %param.22) | copy-start | bytes 12292
  117.2 9.7 %collective-permute-start.1 = (bf16[8,128,1024]{2,1,0:T(8,128)(2,1)}, bf16[8,128,1024]{2,1,0:T(8,128)(2,1)}, u32[]{:S(2)}, u32[]{:S(2)}) collective-permute-start(bf16[8,128,1024]{2,1,0:T(8,128)(2,1)} %broadcast_select_fusion), channel_id=1, source_target_pairs={{0,128},{128,0},{1,129},{129,1},{2,130},{130,2},{3,131},{131,3},{4... | collective-permute-start | bytes 6291464 | tf_op jit(solution)/shard_map/ppermute | solution.py:120
  119.3 0.8 copy-start.4
  121.0 6.0 %copy-start.34 = (f32[1,1,8,128]{3,2,1,0:T(8,128)S(1)}, f32[1,1,8,128]{3,2,1,0:T(8,128)}, u32[]{:S(2)}) copy-start(f32[1,1,8,128]{3,2,1,0:T(8,128)} %param.21) | copy-start | bytes 12292
  155.4 0.6 copy-start.11
  168.2 2.7 copy-start.12
  300.8 0.7 copy-start.21
  301.0 13.6 %copy-start.3 = (f32[768,768]{1,0:T(8,128)}, f32[768,768]{1,0:T(8,128)S(1)}, u32[]{:S(2)}) copy-start(f32[768,768]{1,0:T(8,128)S(1)} %select_select_fusion) | copy-start | bytes 7077892
  301.0 1.8 copy-start.19
  301.6 2.3 copy-start.17
  302.8 2.2 copy-start.15
  303.9 2.2 copy-start.14
  305.0 2.2 copy-start.13
  307.2 2.1 copy-start.2
  314.6 3.4 copy-start.5
  314.6 3.4 copy-start.24
  316.2 3.8 copy-start.26
  319.0 2.4 collective-permute-start.2
  321.4 0.8 copy-start.7
  321.4 0.9 copy-start.8
  325.2 1.0 copy-start.6
  373.7 40.4 %copy-start.22 = (pred[128,128]{1,0:T(8,128)(4,1)S(1)}, pred[128,128]{1,0:T(8,128)(4,1)}, u32[]{:S(2)}) copy-start(pred[128,128]{1,0:T(8,128)(4,1)} %get-tuple-element.61) | copy-start | bytes 49156
  413.8 1.3 copy-start.20
  413.9 2.0 copy-start.18
  414.6 2.1 copy-start.16
  429.7 7.2 %copy-start.10 = (bf16[1,1,1024,128]{3,2,1,0:T(8,128)(2,1)S(1)}, bf16[1,1,1024,128]{3,2,1,0:T(8,128)(2,1)}, u32[]{:S(2)}) copy-start(bf16[1,1,1024,128]{3,2,1,0:T(8,128)(2,1)} %param.24) | copy-start | bytes 786436
  436.8 11.5 %copy-start.31 = (pred[4]{0:T(512)(128)(4,1)S(1)}, pred[4]{0:T(512)(128)(4,1)}, u32[]{:S(2)}) copy-start(pred[4]{0:T(512)(128)(4,1)} %get-tuple-element.72) | copy-start | bytes 16
  437.3 1.4 collective-permute-start.3
  439.5 16.9 %copy-start.30 = (pred[4]{0:T(512)(128)(4,1)S(1)}, pred[4]{0:T(512)(128)(4,1)}, u32[]{:S(2)}) copy-start(pred[4]{0:T(512)(128)(4,1)} %get-tuple-element.71) | copy-start | bytes 16
  439.5 4.8 collective-permute-start.4
  441.1 6.4 %collective-permute-start.5 = (f32[128,129]{0,1:T(8,128)S(1)}, f32[128,129]{0,1:T(8,128)S(1)}, u32[]{:S(2)}, u32[]{:S(2)}) collective-permute-start(f32[128,129]{0,1:T(8,128)S(1)} %fusion.392), channel_id=1, source_target_pairs={{0,64},{32,96},{64,0},{96,32},{1,65},{33,97},{65,1},{97,33},{2,66}... | collective-permute-start | bytes 198152 | tf_op jit(solution)/shard_map/ppermute | solution.py:34
  442.2 5.4 %collective-permute-start.6 = (f32[128,129]{0,1:T(8,128)S(1)}, f32[128,129]{0,1:T(8,128)S(1)}, u32[]{:S(2)}, u32[]{:S(2)}) collective-permute-start(f32[128,129]{0,1:T(8,128)S(1)} %fusion.392), channel_id=1, source_target_pairs={{0,96},{32,0},{64,32},{96,64},{1,97},{33,1},{65,33},{97,65},{2,98}... | collective-permute-start | bytes 198152 | tf_op jit(solution)/shard_map/ppermute | solution.py:34
  448.4 6.3 %collective-permute-start.7 = (f32[128,129]{0,1:T(8,128)S(1)}, f32[128,129]{0,1:T(8,128)S(1)}, u32[]{:S(2)}, u32[]{:S(2)}) collective-permute-start(f32[128,129]{0,1:T(8,128)S(1)} %fusion.391), channel_id=1, source_target_pairs={{0,1},{1,2},{2,3},{3,0},{4,5},{5,6},{6,7},{7,4},{8,9},{9,10},{10,1... | collective-permute-start | bytes 198152 | tf_op jit(solution)/shard_map/ppermute | solution.py:34
  448.7 6.1 %collective-permute-start.8 = (f32[128,129]{0,1:T(8,128)S(1)}, f32[128,129]{0,1:T(8,128)S(1)}, u32[]{:S(2)}, u32[]{:S(2)}) collective-permute-start(f32[128,129]{0,1:T(8,128)S(1)} %fusion.391), channel_id=1, source_target_pairs={{0,2},{1,3},{2,0},{3,1},{4,6},{5,7},{6,4},{7,5},{8,10},{9,11},{10,... | collective-permute-start | bytes 198152 | tf_op jit(solution)/shard_map/ppermute | solution.py:34
  450.8 4.8 collective-permute-start.9
  456.5 10.4 %collective-permute-start.10 = (f32[128,129]{0,1:T(8,128)S(1)}, f32[128,129]{0,1:T(8,128)S(1)}, u32[]{:S(2)}, u32[]{:S(2)}) collective-permute-start(f32[128,129]{0,1:T(8,128)S(1)} %bitcast.292), channel_id=1, source_target_pairs={{0,4},{1,5},{2,6},{3,7},{4,8},{5,9},{6,10},{7,11},{8,12},{9,13},{1... | collective-permute-start | bytes 198152 | tf_op jit(solution)/shard_map/ppermute | solution.py:34
  456.6 13.7 %collective-permute-start.11 = (f32[128,129]{0,1:T(8,128)S(1)}, f32[128,129]{0,1:T(8,128)S(1)}, u32[]{:S(2)}, u32[]{:S(2)}) collective-permute-start(f32[128,129]{0,1:T(8,128)S(1)} %bitcast.293), channel_id=1, source_target_pairs={{0,8},{1,9},{2,10},{3,11},{4,12},{5,13},{6,14},{7,15},{8,16},{9,17... | collective-permute-start | bytes 198152 | tf_op jit(solution)/shard_map/ppermute | solution.py:34
  460.2 11.0 %collective-permute-start.12 = (f32[128,129]{0,1:T(8,128)S(1)}, f32[128,129]{0,1:T(8,128)S(1)}, u32[]{:S(2)}, u32[]{:S(2)}) collective-permute-start(f32[128,129]{0,1:T(8,128)S(1)} %bitcast.294), channel_id=1, source_target_pairs={{0,12},{1,13},{2,14},{3,15},{4,16},{5,17},{6,18},{7,19},{8,20},{9,... | collective-permute-start | bytes 198152 | tf_op jit(solution)/shard_map/ppermute | solution.py:34
  461.8 9.5 %collective-permute-start.13 = (f32[128,129]{0,1:T(8,128)S(1)}, f32[128,129]{0,1:T(8,128)S(1)}, u32[]{:S(2)}, u32[]{:S(2)}) collective-permute-start(f32[128,129]{0,1:T(8,128)S(1)} %bitcast.295), channel_id=1, source_target_pairs={{0,16},{1,17},{2,18},{3,19},{4,20},{5,21},{6,22},{7,23},{8,24},{9,... | collective-permute-start | bytes 198152 | tf_op jit(solution)/shard_map/ppermute | solution.py:34
  464.7 9.8 %collective-permute-start.14 = (f32[128,129]{0,1:T(8,128)S(1)}, f32[128,129]{0,1:T(8,128)S(1)}, u32[]{:S(2)}, u32[]{:S(2)}) collective-permute-start(f32[128,129]{0,1:T(8,128)S(1)} %bitcast.296), channel_id=1, source_target_pairs={{0,20},{1,21},{2,22},{3,23},{4,24},{5,25},{6,26},{7,27},{8,28},{9,... | collective-permute-start | bytes 198152 | tf_op jit(solution)/shard_map/ppermute | solution.py:34
  466.9 8.9 %collective-permute-start.15 = (f32[128,129]{0,1:T(8,128)S(1)}, f32[128,129]{0,1:T(8,128)S(1)}, u32[]{:S(2)}, u32[]{:S(2)}) collective-permute-start(f32[128,129]{0,1:T(8,128)S(1)} %bitcast.297), channel_id=1, source_target_pairs={{0,24},{1,25},{2,26},{3,27},{4,28},{5,29},{6,30},{7,31},{8,0},{9,1... | collective-permute-start | bytes 198152 | tf_op jit(solution)/shard_map/ppermute | solution.py:34
  470.3 6.0 %collective-permute-start.16 = (f32[128,129]{0,1:T(8,128)S(1)}, f32[128,129]{0,1:T(8,128)S(1)}, u32[]{:S(2)}, u32[]{:S(2)}) collective-permute-start(f32[128,129]{0,1:T(8,128)S(1)} %bitcast.298), channel_id=1, source_target_pairs={{0,28},{1,29},{2,30},{3,31},{4,0},{5,1},{6,2},{7,3},{8,4},{9,5},{1... | collective-permute-start | bytes 198152 | tf_op jit(solution)/shard_map/ppermute | solution.py:34
  476.9 0.7 copy-start.28
  476.9 25.3 %copy-start.1 = (bf16[2,128,1024]{2,1,0:T(8,128)(2,1)S(1)}, bf16[2,128,1024]{2,1,0:T(8,128)(2,1)}, u32[]{:S(2)}) copy-start(bf16[2,128,1024]{2,1,0:T(8,128)(2,1)} %param.19) | copy-start | bytes 1572868
  477.3 23.6 %copy-start.32 = (f32[128]{0:T(128)S(1)}, f32[128]{0:T(128)}, u32[]{:S(2)}) copy-start(f32[128]{0:T(128)} %param.27) | copy-start | bytes 1540
  501.2 1.1 copy-start.29
Sparse Core Ops, SparseCore 0:
  10.6 100.8 all-gather.1

commit v5 on v4

--- a/solution.py
+++ b/solution.py
@@ -51,15 +51,14 @@
 BLOCK = 128
 
 
-def diagonal_inverses(lower):
-    blocks = lower.shape[0] // BLOCK
-    diag = jnp.stack([lower[i * BLOCK:(i + 1) * BLOCK, i * BLOCK:(i + 1) * BLOCK] for i in range(blocks)])
-    row = lax.broadcasted_iota(jnp.int32, (BLOCK, BLOCK), 0)
-    col = lax.broadcasted_iota(jnp.int32, (BLOCK, BLOCK), 1)
-    eye = (row == col).astype(lower.dtype)
+def triangular_inverses(diag):
+    size_of = diag.shape[-1]
+    row = lax.broadcasted_iota(jnp.int32, (size_of, size_of), 0)
+    col = lax.broadcasted_iota(jnp.int32, (size_of, size_of), 1)
+    eye = (row == col).astype(diag.dtype)
     inverse = eye / jnp.sum(diag * eye, axis=-1, keepdims=True)
     size = 1
-    while size < BLOCK:
+    while size < size_of:
         below = (row // (2 * size) == col // (2 * size)) & ((row // size) % 2 == 1) & ((col // size) % 2 == 0)
         off = jnp.where(below, diag, 0.0)
         inverse = inverse - jnp.matmul(
@@ -67,6 +66,26 @@
         )
         size *= 2
     return inverse
+
+
+def blocked_cholesky(matrix):
+    order = matrix.shape[0]
+    blocks = order // BLOCK
+    trailing = matrix
+    columns = []
+    inverses = []
+    for k in range(blocks):
+        factor = lax.linalg.cholesky(trailing[:BLOCK, :BLOCK])
+        inverse = triangular_inverses(factor)
+        inverses.append(inverse)
+        if k < blocks - 1:
+            panel = jnp.dot(trailing[BLOCK:, :BLOCK], inverse.T, precision=highest)
+            trailing = trailing[BLOCK:, BLOCK:] - jnp.dot(panel, panel.T, precision=highest)
+            column = jnp.concatenate([factor, panel], axis=0)
+        else:
+            column = factor
+        columns.append(jnp.pad(column, ((k * BLOCK, 0), (0, 0))))
+    return jnp.concatenate(columns, axis=1), jnp.stack(inverses)
 
 
 def forward_solve(lower, inverses, rhs):
@@ -122,6 +141,7 @@
     selected = jnp.where((block_ids % 2 == shard)[:, None, None], own, from_partner)
     end_factor = jnp.where((shard == 0) | (shard == shards - 1), 1.0, 2.0).astype(jnp.float32)
     hessian = period_hessian(selected, line_weight[0, 0], barrier[0, 0], ramp_weight, end_factor)
+    hessian = (hessian + hessian.T) / 2
 
     link_float = link_columns[0, 0].astype(jnp.float32)
     rhs = jnp.concatenate([gradient[0, 0][:, None], link_float], axis=1)
@@ -129,8 +149,7 @@
     h_nn = hessian[count:, count:]
     h_nr = hessian[count:, :count]
     h_rr = hessian[:count, :count]
-    l_nn = lax.linalg.cholesky(h_nn)
-    inv_nn = diagonal_inverses(l_nn)
+    l_nn, inv_nn = blocked_cholesky(h_nn)
     solved = forward_solve(l_nn, inv_nn, jnp.concatenate([h_nr, rhs[count:]], axis=1))
     x_nr = solved[:, :count]
     y_n = solved[:, count:]
@@ -150,8 +169,7 @@
         ],
         axis=0,
     )
-    lower = lax.linalg.cholesky(system)
-    inv_sys = diagonal_inverses(lower)
+    lower, inv_sys = blocked_cholesky(system)
     ramp_both = backward_solve(
         lower,
         inv_sys,
@@ -170,8 +188,10 @@
     inverse_count = 1.0 / (shards * lax.axis_size("scen") * lax.axis_size("line"))
     link_system = jnp.diag(link_diag) + inverse_count * mat_total
     right_side = inverse_count * vec_total - link_rhs
-    link_lower = jnp.linalg.cholesky(link_system)
-    link_step = jax.scipy.linalg.cho_solve((link_lower, True), right_side)
+    link_lower, link_inv = blocked_cholesky(link_system)
+    link_step = backward_solve(
+        link_lower, link_inv, forward_solve(link_lower, link_inv, right_side[:, None])
+    )[:, 0]
     newton_step = step_vec - jnp.dot(step_cols, link_step, precision=highest)
     return (newton_step[None, None], link_step)
 

time: 517 us -> 465 us (0.90)
  other arithmetic: 250 us -> 156 us
  matrix products: 65.3 us -> 107 us
    another operation x42 -> x33, other arithmetic: 236 us -> 137 us  [blocked_cholesky(): factor = lax.linalg.cholesky(trailing[:BLOCK, :BLOCK])]
    dot_general x28 -> x170, matrix products: 13.2 us -> 78.9 us  [the longest x77 44.7 us: triangular_inverses(): jnp.matmul(inverse, off, precision=highest)]
    another operation x18 -> x0, matrix products: 18.3 us -> none  [the longest x10 12.5 us: on_device(): l_nn = lax.linalg.cholesky(h_nn)]
    dot_general x0 -> x9, local copies, waits for them, and re-layouts: none -> 10.8 us  [the longest x1 5.87 us: period_hessian(): lax.dot_general(flat, scaled_flat, (((0,), (0,)), ((), ())), preferred_el...]
    reduce_sum x2 -> x11, other arithmetic: 0.32 us -> 7.46 us  [triangular_inverses(): inverse = eye / jnp.sum(diag * eye, axis=-1, keepdims=True)]
    another operation x20 -> x11, local copies, waits for them, and re-layouts: 6.99 us -> 1.68 us  [blocked_cholesky(): factor = lax.linalg.cholesky(trailing[:BLOCK, :BLOCK])]
  transfers between devices with their start and end apart: 18 -> 18, of which waited for: 11 -> 12; matrix products, arithmetic and copies ran while one was open for 2% -> 1% of each run, Pallas kernels for 0% -> 0%
where the time goes in v5:
time: 465 us; the launch traced here: 457 us
  other arithmetic  156 us (34%)
  waiting for transfers between devices  117 us (25%)
  matrix products  107 us (23%)
  local copies, waits for them, and re-layouts  34.9 us (8%)
  starting transfers between devices  23.9 us (5%)
  between operations  18.1 us (4%)
    another operation x33, other arithmetic, blocked_cholesky(): factor = lax.linalg.cholesky(trailing[:BLOCK, :BLOCK])  137 us
    all_gather x1, waiting for transfers between devices, on_device(): half = lax.all_gather(mine_half, 'line', axis=0, tiled=True)  101 us
    dot_general x77, matrix products, triangular_inverses(): jnp.matmul(inverse, off, precision=highest)  44.7 us
    ppermute x14, starting transfers between devices, group_sum(): received.append(lax.ppermute(value, axis, pairs))  23 us
    dot_general x77, matrix products, triangular_inverses(): jnp.matmul(jnp.matmul(inverse, off, precision=highest), inverse, precisio...  20.4 us
    ppermute x14, waiting for transfers between devices, group_sum(): received.append(lax.ppermute(value, axis, pairs))  14 us
  transfers between devices with their start and end apart: 18, of which 12 were waited for; matrix products, arithmetic and copies ran while one was open for 1% of the time, Pallas kernels for 0%

profile of v5, /device:TPU:2, one launch (start us, length us, event | category | flops | bytes accessed | tf_op | source)
XLA Modules:
  0.0 457.2 jit_solution(5118136300887878448)
XLA Ops:
  9.3 1.1 collective-permute-done
  10.4 101.1 %all-gather.2.cloned.1.call-done = bf16[32,128,1024]{2,1,0:T(8,128)(2,1)} async-done(((bf16[1,128,1024]{2,1,0:T(8,128)(2,1)}), bf16[32,128,1024]{2,1,0:T(8,128)(2,1)}) %all-gather.2.cloned.1.call-update) | async-done | bytes 8388624 | tf_op jit(solution)/shard_map/all_gather | solution.py:135
  111.4 4.1 gather_fusion.3
  115.6 1.7 broadcast_select_fusion
  118.7 4.1 gather_fusion.2
  122.8 6.9 %fusion.2 = f32[1024,1024,1]{1,0,2:T(8,128)} fusion(bf16[8,128,1024]{2,1,0:T(8,128)(2,1)} %collective-permute-done.1, bf16[8,128,1024]{2,1,0:T(8,128)(2,1)S(1)} %gather_fusion.2, f32[8,128]{1,0:T(8,128)S(1)} %bitcast.428, pred[8]{0:T(512)(128)(4,1)S(1)} %get-tuple-element.23, pred[8]{0:T(512)(128)(4,1)S(1)} %get-tuple-element.45), kind=kOutput, calls=%fused_computation.12 | convolution fusion | flops 2154823680 | bytes 8392720 | tf_op jit(solution)/shard_map/dot_general | solution.py:14
  129.7 5.9 %copy.148 = f32[1024,1024]{0,1:T(8,128)} copy(f32[1024,1024]{1,0:T(8,128)} %bitcast.403) | data formatting | bytes 8388608 | tf_op jit(solution)/shard_map/dot_general | solution.py:14
  135.5 4.5 fusion.1
  140.1 2.0 copy-done.2
  143.1 11.7 %custom-call.13 = f32[128,128]{1,0:T(8,128)S(1)} custom-call(f32[128,128]{1,0:T(8,128)S(1)} %copy.151), custom_call_target="Cholesky" | custom-call | tf_op jit(solution)/shard_map/cholesky/custom-call.1 | solution.py:78
  155.0 1.2 slice.365
  162.8 1.7 fusion.38
  164.5 2.9 slice_subtract_fusion
  167.6 11.9 %custom-call.14 = f32[128,128]{1,0:T(8,128)S(1)} custom-call(f32[128,128]{1,0:T(8,128)S(1)} %copy.164), custom_call_target="Cholesky" | custom-call | tf_op jit(solution)/shard_map/cholesky/custom-call.1 | solution.py:78
  186.9 1.0 convolution_subtract_fusion
  188.2 11.7 %custom-call.15 = f32[128,128]{1,0:T(8,128)S(1)} custom-call(f32[128,128]{1,0:T(8,128)S(1)} %copy.176), custom_call_target="Cholesky" | custom-call | tf_op jit(solution)/shard_map/cholesky/custom-call.1 | solution.py:78
  209.3 11.7 %custom-call.16 = f32[128,128]{1,0:T(8,128)S(1)} custom-call(f32[128,128]{1,0:T(8,128)S(1)} %copy.190), custom_call_target="Cholesky" | custom-call | tf_op jit(solution)/shard_map/cholesky/custom-call.1 | solution.py:78
  229.0 12.1 %custom-call.17 = f32[128,128]{1,0:T(8,128)S(1)} custom-call(f32[128,128]{1,0:T(8,128)S(1)} %copy.203), custom_call_target="Cholesky" | custom-call | tf_op jit(solution)/shard_map/cholesky/custom-call.1 | solution.py:78
  248.9 11.7 %custom-call.18 = f32[128,128]{1,0:T(8,128)S(1)} custom-call(f32[128,128]{1,0:T(8,128)S(1)} %copy.216), custom_call_target="Cholesky" | custom-call | tf_op jit(solution)/shard_map/cholesky/custom-call.1 | solution.py:78
  262.2 1.3 constant_dynamic-update-slice_fusion.7
  266.7 1.2 fusion.261
  268.3 1.0 fusion.259
  269.6 1.1 fusion.257
  271.0 1.1 fusion.255
  272.4 1.0 fusion.253
  273.8 1.0 fusion.251
  279.5 1.1 fusion.36
  282.0 1.8 slice_subtract_fusion.1
  284.7 1.3 collective-permute-done.2
  287.1 11.7 %custom-call.19 = f32[128,128]{1,0:T(8,128)S(1)} custom-call(f32[128,128]{1,0:T(8,128)S(1)} %copy.228), custom_call_target="Cholesky" | custom-call | tf_op jit(solution)/shard_map/cholesky/custom-call.1 | solution.py:78
  306.7 1.5 fusion.26
  310.1 12.1 %custom-call.20 = f32[128,128]{1,0:T(8,128)S(1)} custom-call(f32[128,128]{1,0:T(8,128)S(1)} %copy.240), custom_call_target="Cholesky" | custom-call | tf_op jit(solution)/shard_map/cholesky/custom-call.1 | solution.py:78
  328.4 1.3 fusion.110
  329.7 1.3 convolution_subtract_fusion.3
  331.2 11.7 %custom-call.21 = f32[128,128]{1,0:T(8,128)S(1)} custom-call(f32[128,128]{1,0:T(8,128)S(1)} %copy.252), custom_call_target="Cholesky" | custom-call | tf_op jit(solution)/shard_map/cholesky/custom-call.1 | solution.py:78
  349.8 11.9 %custom-call.22 = f32[128,128]{1,0:T(8,128)S(1)} custom-call(f32[128,128]{1,0:T(8,128)S(1)} %fusion.159), custom_call_target="Cholesky" | custom-call | tf_op jit(solution)/shard_map/cholesky/custom-call.1 | solution.py:78
  366.3 1.0 fusion.205
  367.6 1.0 fusion.203
  368.9 1.0 fusion.201
  370.3 1.1 fusion.199
  371.7 1.1 fusion.197
  373.0 1.1 fusion.195
  375.3 1.2 fusion.119
  376.9 1.2 fusion.118
  388.2 2.4 collective-permute-start.5
  390.6 1.8 collective-permute-start.4
  392.4 2.1 collective-permute-done.5
  397.0 1.5 collective-permute-start.8
  399.1 1.4 collective-permute-done.9
  400.5 2.6 collective-permute-done.8
  404.8 3.6 collective-permute-start.11
  408.4 1.6 collective-permute-start.12
  410.0 2.9 collective-permute-start.13
  412.9 2.2 collective-permute-start.14
  415.1 3.4 collective-permute-start.15
  419.6 3.8 collective-permute-done.14
  423.7 1.1 collective-permute-done.16
  425.8 11.7 %custom-call.23 = f32[128,128]{1,0:T(8,128)S(1)} custom-call(f32[128,128]{1,0:T(8,128)S(1)} %fusion.158), custom_call_target="Cholesky" | custom-call | tf_op jit(solution)/shard_map/cholesky/custom-call.1 | solution.py:78
  440.3 1.0 fusion.191
  441.7 1.0 fusion.189
  443.0 1.1 fusion.187
  444.5 1.0 fusion.185
  445.8 1.0 fusion.183
  447.2 1.0 fusion.181
  (625 shorter events, 109.7 us)
Async XLA Ops:
  7.2 104.3 %all-gather.2.cloned.1.call-start = ((), (), s32[]{:S(2)}) async-start(), calls=%async_computation | async-start | bytes 8650752 | tf_op jit(solution)/shard_map/all_gather | solution.py:135
  9.0 1.4 collective-permute-start
  9.1 238.3 %copy-start.120 = (pred[128]{0:T(512)(128)(4,1)}, pred[128]{0:T(512)(128)(4,1)S(1)}, u32[]{:S(2)}) copy-start(pred[128]{0:T(512)(128)(4,1)S(1)} %compare_and_fusion.6) | copy-start | bytes 388
  9.2 234.7 %copy-start.68 = (s32[128]{0:T(128)}, s32[128]{0:T(128)S(1)}, u32[]{:S(2)}) copy-start(s32[128]{0:T(128)S(1)} %get-tuple-element.52) | copy-start | bytes 1540
  9.2 234.7 %copy-start.72 = (s32[128]{0:T(128)}, s32[128]{0:T(128)S(1)}, u32[]{:S(2)}) copy-start(s32[128]{0:T(128)S(1)} %get-tuple-element.53) | copy-start | bytes 1540
  9.2 234.7 %copy-start.76 = (pred[128]{0:T(512)(128)(4,1)}, pred[128]{0:T(512)(128)(4,1)S(1)}, u32[]{:S(2)}) copy-start(pred[128]{0:T(512)(128)(4,1)S(1)} %get-tuple-element.55) | copy-start | bytes 388
  117.3 5.5 %collective-permute-start.1 = (bf16[8,128,1024]{2,1,0:T(8,128)(2,1)}, bf16[8,128,1024]{2,1,0:T(8,128)(2,1)}, u32[]{:S(2)}, u32[]{:S(2)}) collective-permute-start(bf16[8,128,1024]{2,1,0:T(8,128)(2,1)} %broadcast_select_fusion), channel_id=1, source_target_pairs={{0,128},{128,0},{1,129},{129,1},{2,130},{130,2},{3,131},{131,3},{4... | collective-permute-start | bytes 6291464 | tf_op jit(solution)/shard_map/ppermute | solution.py:139
  117.5 128.5 %copy-start.112 = (s32[128]{0:T(128)}, s32[128]{0:T(128)S(1)}, u32[]{:S(2)}) copy-start(s32[128]{0:T(128)S(1)} %get-tuple-element.62) | copy-start | bytes 1540
  117.5 128.5 %copy-start.116 = (s32[128]{0:T(128)}, s32[128]{0:T(128)S(1)}, u32[]{:S(2)}) copy-start(s32[128]{0:T(128)S(1)} %get-tuple-element.63) | copy-start | bytes 1540
  117.5 129.2 %copy-start.100 = (s32[128]{0:T(128)}, s32[128]{0:T(128)S(1)}, u32[]{:S(2)}) copy-start(s32[128]{0:T(128)S(1)} %get-tuple-element.64) | copy-start | bytes 1540
  117.5 129.2 %copy-start.104 = (s32[128]{0:T(128)}, s32[128]{0:T(128)S(1)}, u32[]{:S(2)}) copy-start(s32[128]{0:T(128)S(1)} %get-tuple-element.65) | copy-start | bytes 1540
  117.6 129.1 %copy-start.108 = (pred[128]{0:T(512)(128)(4,1)}, pred[128]{0:T(512)(128)(4,1)S(1)}, u32[]{:S(2)}) copy-start(pred[128]{0:T(512)(128)(4,1)S(1)} %get-tuple-element.67) | copy-start | bytes 388
  117.6 129.8 %copy-start.80 = (pred[128]{0:T(512)(128)(4,1)}, pred[128]{0:T(512)(128)(4,1)S(1)}, u32[]{:S(2)}) copy-start(pred[128]{0:T(512)(128)(4,1)S(1)} %get-tuple-element.66) | copy-start | bytes 388
  117.6 129.8 %copy-start.84 = (s32[128]{0:T(128)}, s32[128]{0:T(128)S(1)}, u32[]{:S(2)}) copy-start(s32[128]{0:T(128)S(1)} %get-tuple-element.68) | copy-start | bytes 1540
  117.6 129.8 %copy-start.88 = (s32[128]{0:T(128)}, s32[128]{0:T(128)S(1)}, u32[]{:S(2)}) copy-start(s32[128]{0:T(128)S(1)} %get-tuple-element.69) | copy-start | bytes 1540
  117.6 129.8 %copy-start.92 = (s32[128]{0:T(128)}, s32[128]{0:T(128)S(1)}, u32[]{:S(2)}) copy-start(s32[128]{0:T(128)S(1)} %get-tuple-element.70) | copy-start | bytes 1540
  117.7 129.8 %copy-start.96 = (s32[128]{0:T(128)}, s32[128]{0:T(128)S(1)}, u32[]{:S(2)}) copy-start(s32[128]{0:T(128)S(1)} %get-tuple-element.71) | copy-start | bytes 1540
  167.4 16.0 %copy-start.3 = (f32[640,640]{0,1:T(8,128)}, f32[640,640]{0,1:T(8,128)S(1)}, u32[]{:S(2)}) copy-start(f32[640,640]{0,1:T(8,128)S(1)} %slice_subtract_fusion) | copy-start | bytes 4915204
  187.9 12.1 %copy-start.9 = (f32[512,512]{0,1:T(8,128)}, f32[512,512]{0,1:T(8,128)S(1)}, u32[]{:S(2)}) copy-start(f32[512,512]{0,1:T(8,128)S(1)} %convolution_subtract_fusion) | copy-start | bytes 3145732
  208.4 15.9 %copy-start.5 = (f32[384,128]{1,0:T(8,128)}, f32[384,128]{1,0:T(8,128)S(1)}, u32[]{:S(2)}) copy-start(f32[384,128]{1,0:T(8,128)S(1)} %fusion.100) | copy-start | bytes 589828
  228.0 16.4 %copy-start.18 = (f32[128,128]{0,1:T(8,128)}, f32[128,128]{0,1:T(8,128)S(1)}, u32[]{:S(2)}) copy-start(f32[128,128]{0,1:T(8,128)S(1)} %convolution_subtract_fusion.55) | copy-start | bytes 196612
  228.4 16.7 %copy-start.11 = (f32[256,128]{1,0:T(8,128)}, f32[256,128]{1,0:T(8,128)S(1)}, u32[]{:S(2)}) copy-start(f32[256,128]{1,0:T(8,128)S(1)} %fusion.112) | copy-start | bytes 393220
  248.1 13.3 %copy-start.21 = (f32[128,128]{0,1:T(8,128)}, f32[128,128]{0,1:T(8,128)S(1)}, u32[]{:S(2)}) copy-start(f32[128,128]{0,1:T(8,128)S(1)} %convolution_subtract_fusion.48) | copy-start | bytes 196612
  248.7 16.7 %copy-start.69 = (s32[128]{0:T(128)S(1)}, s32[128]{0:T(128)}, u32[]{:S(2)}) copy-start(s32[128]{0:T(128)} %copy-done.68) | copy-start | bytes 1540
  248.7 16.7 %copy-start.73 = (s32[128]{0:T(128)S(1)}, s32[128]{0:T(128)}, u32[]{:S(2)}) copy-start(s32[128]{0:T(128)} %copy-done.72) | copy-start | bytes 1540
  248.7 16.7 %copy-start.77 = (pred[128]{0:T(512)(128)(4,1)S(1)}, pred[128]{0:T(512)(128)(4,1)}, u32[]{:S(2)}) copy-start(pred[128]{0:T(512)(128)(4,1)} %copy-done.76) | copy-start | bytes 388
  264.0 5.6 %copy-start.113 = (s32[128]{0:T(128)S(1)}, s32[128]{0:T(128)}, u32[]{:S(2)}) copy-start(s32[128]{0:T(128)} %copy-done.112) | copy-start | bytes 1540
  265.4 5.6 %copy-start.101 = (s32[128]{0:T(128)S(1)}, s32[128]{0:T(128)}, u32[]{:S(2)}) copy-start(s32[128]{0:T(128)} %copy-done.100) | copy-start | bytes 1540
  265.4 5.6 %copy-start.105 = (s32[128]{0:T(128)S(1)}, s32[128]{0:T(128)}, u32[]{:S(2)}) copy-start(s32[128]{0:T(128)} %copy-done.104) | copy-start | bytes 1540
  265.4 5.6 %copy-start.109 = (pred[128]{0:T(512)(128)(4,1)S(1)}, pred[128]{0:T(512)(128)(4,1)}, u32[]{:S(2)}) copy-start(pred[128]{0:T(512)(128)(4,1)} %copy-done.108) | copy-start | bytes 388
  266.7 5.7 %copy-start.81 = (pred[128]{0:T(512)(128)(4,1)S(1)}, pred[128]{0:T(512)(128)(4,1)}, u32[]{:S(2)}) copy-start(pred[128]{0:T(512)(128)(4,1)} %copy-done.80) | copy-start | bytes 388
  266.7 5.7 %copy-start.85 = (s32[128]{0:T(128)S(1)}, s32[128]{0:T(128)}, u32[]{:S(2)}) copy-start(s32[128]{0:T(128)} %copy-done.84) | copy-start | bytes 1540
  266.7 5.7 %copy-start.89 = (s32[128]{0:T(128)S(1)}, s32[128]{0:T(128)}, u32[]{:S(2)}) copy-start(s32[128]{0:T(128)} %copy-done.88) | copy-start | bytes 1540
  283.9 17.5 %copy-start.70 = (s32[128]{0:T(128)S(1)}, s32[128]{0:T(128)}, u32[]{:S(2)}) copy-start(s32[128]{0:T(128)} %copy-done.68) | copy-start | bytes 1540
  283.9 17.5 %copy-start.74 = (s32[128]{0:T(128)S(1)}, s32[128]{0:T(128)}, u32[]{:S(2)}) copy-start(s32[128]{0:T(128)} %copy-done.72) | copy-start | bytes 1540
  283.9 17.5 %copy-start.78 = (pred[128]{0:T(512)(128)(4,1)S(1)}, pred[128]{0:T(512)(128)(4,1)}, u32[]{:S(2)}) copy-start(pred[128]{0:T(512)(128)(4,1)} %copy-done.76) | copy-start | bytes 388
  283.9 2.2 collective-permute-start.2
  287.0 16.4 %copy-start.114 = (s32[128]{0:T(128)S(1)}, s32[128]{0:T(128)}, u32[]{:S(2)}) copy-start(s32[128]{0:T(128)} %copy-done.112) | copy-start | bytes 1540
  287.0 16.4 %copy-start.118 = (s32[128]{0:T(128)S(1)}, s32[128]{0:T(128)}, u32[]{:S(2)}) copy-start(s32[128]{0:T(128)} %copy-done.116) | copy-start | bytes 1540
  306.2 55.6 %copy-start.24 = (f32[128,128]{0,1:T(8,128)}, f32[128,128]{0,1:T(8,128)S(1)}, u32[]{:S(2)}) copy-start(f32[128,128]{0,1:T(8,128)S(1)} %convolution_subtract_fusion.34) | copy-start | bytes 196612
  328.3 46.3 %copy-start.32 = (f32[128,128]{0,1:T(8,128)}, f32[128,128]{0,1:T(8,128)S(1)}, u32[]{:S(2)}) copy-start(f32[128,128]{0,1:T(8,128)S(1)} %convolution_subtract_fusion.27) | copy-start | bytes 196612
  349.1 18.5 %copy-start.34 = (f32[128,128]{0,1:T(8,128)}, f32[128,128]{0,1:T(8,128)S(1)}, u32[]{:S(2)}) copy-start(f32[128,128]{0,1:T(8,128)S(1)} %convolution_subtract_fusion.20) | copy-start | bytes 196612
  385.1 19.7 %copy-start.13 = (f32[1024,129]{0,1:T(8,128)}, f32[1024,129]{0,1:T(8,128)S(1)}, u32[]{:S(2)}) copy-start(f32[1024,129]{0,1:T(8,128)S(1)} %constant_dynamic-update-slice_fusion.18) | copy-start | bytes 1585156
  385.5 1.4 collective-permute-start.3
  387.6 4.8 %collective-permute-start.6 = (f32[128,129]{0,1:T(8,128)S(1)}, f32[128,129]{0,1:T(8,128)S(1)}, u32[]{:S(2)}, u32[]{:S(2)}) collective-permute-start(f32[128,129]{0,1:T(8,128)S(1)} %fusion.933), channel_id=1, source_target_pairs={{0,96},{32,0},{64,32},{96,64},{1,97},{33,1},{65,33},{97,65},{2,98}... | collective-permute-start | bytes 198152 | tf_op jit(solution)/shard_map/ppermute | solution.py:34
  388.2 6.3 %collective-permute-start.5 = (f32[128,129]{0,1:T(8,128)S(1)}, f32[128,129]{0,1:T(8,128)S(1)}, u32[]{:S(2)}, u32[]{:S(2)}) collective-permute-start(f32[128,129]{0,1:T(8,128)S(1)} %fusion.933), channel_id=1, source_target_pairs={{0,64},{32,96},{64,0},{96,32},{1,65},{33,97},{65,1},{97,33},{2,66}... | collective-permute-start | bytes 198152 | tf_op jit(solution)/shard_map/ppermute | solution.py:34
  390.6 4.8 %collective-permute-start.4 = (f32[128,129]{0,1:T(8,128)S(1)}, f32[128,129]{0,1:T(8,128)S(1)}, u32[]{:S(2)}, u32[]{:S(2)}) collective-permute-start(f32[128,129]{0,1:T(8,128)S(1)} %fusion.933), channel_id=1, source_target_pairs={{0,32},{32,64},{64,96},{96,0},{1,33},{33,65},{65,97},{97,1},{2,34}... | collective-permute-start | bytes 198152 | tf_op jit(solution)/shard_map/ppermute | solution.py:34
  396.1 4.4 collective-permute-start.9
  397.0 6.0 %collective-permute-start.8 = (f32[128,129]{0,1:T(8,128)S(1)}, f32[128,129]{0,1:T(8,128)S(1)}, u32[]{:S(2)}, u32[]{:S(2)}) collective-permute-start(f32[128,129]{0,1:T(8,128)S(1)} %fusion.932), channel_id=1, source_target_pairs={{0,2},{1,3},{2,0},{3,1},{4,6},{5,7},{6,4},{7,5},{8,10},{9,11},{10,... | collective-permute-start | bytes 198152 | tf_op jit(solution)/shard_map/ppermute | solution.py:34
  398.4 5.5 %collective-permute-start.7 = (f32[128,129]{0,1:T(8,128)S(1)}, f32[128,129]{0,1:T(8,128)S(1)}, u32[]{:S(2)}, u32[]{:S(2)}) collective-permute-start(f32[128,129]{0,1:T(8,128)S(1)} %fusion.932), channel_id=1, source_target_pairs={{0,1},{1,2},{2,3},{3,0},{4,5},{5,6},{6,7},{7,4},{8,9},{9,10},{10,1... | collective-permute-start | bytes 198152 | tf_op jit(solution)/shard_map/ppermute | solution.py:34
  404.7 10.4 %collective-permute-start.10 = (f32[128,129]{0,1:T(8,128)S(1)}, f32[128,129]{0,1:T(8,128)S(1)}, u32[]{:S(2)}, u32[]{:S(2)}) collective-permute-start(f32[128,129]{0,1:T(8,128)S(1)} %bitcast.406), channel_id=1, source_target_pairs={{0,4},{1,5},{2,6},{3,7},{4,8},{5,9},{6,10},{7,11},{8,12},{9,13},{1... | collective-permute-start | bytes 198152 | tf_op jit(solution)/shard_map/ppermute | solution.py:34
  404.8 13.7 %collective-permute-start.11 = (f32[128,129]{0,1:T(8,128)S(1)}, f32[128,129]{0,1:T(8,128)S(1)}, u32[]{:S(2)}, u32[]{:S(2)}) collective-permute-start(f32[128,129]{0,1:T(8,128)S(1)} %bitcast.407), channel_id=1, source_target_pairs={{0,8},{1,9},{2,10},{3,11},{4,12},{5,13},{6,14},{7,15},{8,16},{9,17... | collective-permute-start | bytes 198152 | tf_op jit(solution)/shard_map/ppermute | solution.py:34
  408.4 11.1 %collective-permute-start.12 = (f32[128,129]{0,1:T(8,128)S(1)}, f32[128,129]{0,1:T(8,128)S(1)}, u32[]{:S(2)}, u32[]{:S(2)}) collective-permute-start(f32[128,129]{0,1:T(8,128)S(1)} %bitcast.408), channel_id=1, source_target_pairs={{0,12},{1,13},{2,14},{3,15},{4,16},{5,17},{6,18},{7,19},{8,20},{9,... | collective-permute-start | bytes 198152 | tf_op jit(solution)/shard_map/ppermute | solution.py:34
  410.0 9.5 %collective-permute-start.13 = (f32[128,129]{0,1:T(8,128)S(1)}, f32[128,129]{0,1:T(8,128)S(1)}, u32[]{:S(2)}, u32[]{:S(2)}) collective-permute-start(f32[128,129]{0,1:T(8,128)S(1)} %bitcast.409), channel_id=1, source_target_pairs={{0,16},{1,17},{2,18},{3,19},{4,20},{5,21},{6,22},{7,23},{8,24},{9,... | collective-permute-start | bytes 198152 | tf_op jit(solution)/shard_map/ppermute | solution.py:34
  412.9 10.5 %collective-permute-start.14 = (f32[128,129]{0,1:T(8,128)S(1)}, f32[128,129]{0,1:T(8,128)S(1)}, u32[]{:S(2)}, u32[]{:S(2)}) collective-permute-start(f32[128,129]{0,1:T(8,128)S(1)} %bitcast.410), channel_id=1, source_target_pairs={{0,20},{1,21},{2,22},{3,23},{4,24},{5,25},{6,26},{7,27},{8,28},{9,... | collective-permute-start | bytes 198152 | tf_op jit(solution)/shard_map/ppermute | solution.py:34
  415.1 8.6 %collective-permute-start.15 = (f32[128,129]{0,1:T(8,128)S(1)}, f32[128,129]{0,1:T(8,128)S(1)}, u32[]{:S(2)}, u32[]{:S(2)}) collective-permute-start(f32[128,129]{0,1:T(8,128)S(1)} %bitcast.411), channel_id=1, source_target_pairs={{0,24},{1,25},{2,26},{3,27},{4,28},{5,29},{6,30},{7,31},{8,0},{9,1... | collective-permute-start | bytes 198152 | tf_op jit(solution)/shard_map/ppermute | solution.py:34
  418.5 6.3 %collective-permute-start.16 = (f32[128,129]{0,1:T(8,128)S(1)}, f32[128,129]{0,1:T(8,128)S(1)}, u32[]{:S(2)}, u32[]{:S(2)}) collective-permute-start(f32[128,129]{0,1:T(8,128)S(1)} %bitcast.412), channel_id=1, source_target_pairs={{0,28},{1,29},{2,30},{3,31},{4,0},{5,1},{6,2},{7,3},{8,4},{9,5},{1... | collective-permute-start | bytes 198152 | tf_op jit(solution)/shard_map/ppermute | solution.py:34
  424.8 14.1 %copy-start.71 = (s32[128]{0:T(128)S(1)}, s32[128]{0:T(128)}, u32[]{:S(2)}) copy-start(s32[128]{0:T(128)} %copy-done.68) | copy-start | bytes 1540
  424.8 14.1 %copy-start.75 = (s32[128]{0:T(128)S(1)}, s32[128]{0:T(128)}, u32[]{:S(2)}) copy-start(s32[128]{0:T(128)} %copy-done.72) | copy-start | bytes 1540
  424.8 14.1 %copy-start.79 = (pred[128]{0:T(512)(128)(4,1)S(1)}, pred[128]{0:T(512)(128)(4,1)}, u32[]{:S(2)}) copy-start(pred[128]{0:T(512)(128)(4,1)} %copy-done.76) | copy-start | bytes 388
  425.6 17.4 %copy-start.115 = (s32[128]{0:T(128)S(1)}, s32[128]{0:T(128)}, u32[]{:S(2)}) copy-start(s32[128]{0:T(128)} %copy-done.112) | copy-start | bytes 1540
  425.6 17.4 %copy-start.119 = (s32[128]{0:T(128)S(1)}, s32[128]{0:T(128)}, u32[]{:S(2)}) copy-start(s32[128]{0:T(128)} %copy-done.116) | copy-start | bytes 1540
  443.0 5.8 %copy-start.14 = (f32[1024,129]{0,1:T(8,128)S(1)}, f32[1024,129]{0,1:T(8,128)}, u32[]{:S(2)}) copy-start(f32[1024,129]{0,1:T(8,128)} %copy-done.13) | copy-start | bytes 1585156
  443.0 6.9 %copy-start.1 = (bf16[2,128,1024]{2,1,0:T(8,128)(2,1)S(1)}, bf16[2,128,1024]{2,1,0:T(8,128)(2,1)}, u32[]{:S(2)}) copy-start(bf16[2,128,1024]{2,1,0:T(8,128)(2,1)} %param.14) | copy-start | bytes 1572868
  (78 other events, 263.0 us)
Sparse Core Ops, SparseCore 0:
  10.6 100.8 all-gather.1
